TPU v7x, 32 devices: a whole 2x2x4 slice. The times are simulated.
32 devices in a mesh: slab: 16 (over z, x, core), energy: 2 (over y).
Axes of the slice: x: 2, y: 2, z: 4, core: 2. Of those that a mesh axis runs over, the one named last changes fastest.
Arguments:
- mode_floor: float32 [1024], replicated, may hold values from -2.5 to 2.5
- onsite_noise: float32 [256, 1024], P('slab'), may hold values from -0.4 to 0.4
- hopping: float32 [256, 1024], P('slab'), may hold values from 2.3 to 2.7
- lengths: int32 [16], replicated, may hold values from 1 to 16, 128 in all
- energy_index: int32 [8], P('energy'), may hold values from 0 to 4095
- weight_code: int32 [8], P('energy'), may hold values from 1 to 63
- lead_shift: float32 [8, 2, 1024], P('energy'), may hold values from -0.5 to 0.5
- lead_width: float32 [8, 2, 1024], P('energy'), may hold values from 0.2 to 1.2
Outputs:
- density: float32 [256, 1024], P('slab', 'energy')
- bond_density: float32 [256, 1024], P('slab', 'energy')
Inputs may be any that keep to these rules, and one draw needn't show every extreme that they name: `lengths`: entry d counts the slabs of index d of slab, which fill its first slots; the entries sum to 128.
All inputs are finite; a program needn't handle non-finite values.
Results may differ from a plain program's by a relative error of at most 0.029.
Values sent between devices are 32-bit elements; how exact they have to be, the bound alone decides.
No kernel may reach another device: no remote copies, remote signals or barrier semaphores. Data moves between devices by JAX's collectives and lax.ppermute only.
A program may use at most 64 MiB of HBM per device.

v0:
```python
import functools

import jax
import jax.numpy as jnp
from jax import lax
from jax.experimental import pallas as pl
from jax.experimental.pallas import tpu as pltpu
from jax.sharding import PartitionSpec as P

broaden = 0.002
e_low = -1.5
e_step = 3.0 / 4096.0
inv_pi = 1.0 / 3.141592653589793


def reciprocal(real_part, imag_part):
    scale = 1.0 / (real_part * real_part + imag_part * imag_part)
    return (real_part * scale, -imag_part * scale)


def complex_mul(first_re, first_im, second_re, second_im):
    return (
        first_re * second_re - first_im * second_im,
        first_re * second_im + first_im * second_re,
    )


def join_segments(left, right):
    square = left[6] * left[6]
    mix_re, mix_im = complex_mul(left[4], left[5], right[0], right[1])
    inv_re, inv_im = reciprocal(1.0 - square * mix_re, -square * mix_im)
    left_sq_re, left_sq_im = complex_mul(left[2], left[3], left[2], left[3])
    head_re, head_im = complex_mul(left_sq_re, left_sq_im, right[0], right[1])
    head_re, head_im = complex_mul(head_re, head_im, inv_re, inv_im)
    right_sq_re, right_sq_im = complex_mul(right[2], right[3], right[2], right[3])
    tail_re, tail_im = complex_mul(right_sq_re, right_sq_im, left[4], left[5])
    tail_re, tail_im = complex_mul(tail_re, tail_im, inv_re, inv_im)
    link_re, link_im = complex_mul(left[2], left[3], right[2], right[3])
    link_re, link_im = complex_mul(link_re, link_im, inv_re, inv_im)
    return (
        left[0] + square * head_re,
        left[1] + square * head_im,
        left[6] * link_re,
        left[6] * link_im,
        right[4] + square * tail_re,
        right[5] + square * tail_im,
        right[6],
    )


def onsite_terms(table_ref, energy_ref, here, count, devices, slots, points, slot):
    rows = 2 * slots
    levels = table_ref[slot]
    first_on = jnp.logical_and(here == 0, slot == 0).astype(jnp.float32)
    last_on = jnp.logical_and(here == devices - 1, slot == count - 1).astype(jnp.float32)
    onsite_re, onsite_im = [], []
    for point in range(points):
        energy = e_low + e_step * energy_ref[point].astype(jnp.float32)
        onsite_re.append(
            energy - levels
            - first_on * table_ref[rows + 2 * point]
            - last_on * table_ref[rows + 2 * point + 1]
        )
        onsite_im.append(
            broaden
            + first_on * table_ref[rows + 2 * points + 2 * point]
            + last_on * table_ref[rows + 2 * points + 2 * point + 1]
        )
    return jnp.stack(onsite_re), jnp.stack(onsite_im)


def summary_kernel(here_ref, length_ref, energy_ref, table_ref, out_ref, *, slots, points, devices):
    here = here_ref[0]
    count = length_ref[here]

    def single(slot):
        onsite_re, onsite_im = onsite_terms(
            table_ref, energy_ref, here, count, devices, slots, points, slot
        )
        g_re, g_im = reciprocal(onsite_re, onsite_im)
        return (g_re, g_im, g_re, g_im, g_re, g_im, table_ref[slots + slot])

    def body(slot, summary):
        return join_segments(summary, single(slot))

    first_re, first_im, cross_re, cross_im, final_re, final_im, coupling = lax.fori_loop(
        1, count, body, single(0)
    )
    square = coupling * coupling
    sq_re, sq_im = complex_mul(cross_re, cross_im, cross_re, cross_im)
    fields = (first_re, first_im, square * final_re, square * final_im, square * sq_re, square * sq_im)
    for index, value in enumerate(fields):
        out_ref[index * points:(index + 1) * points] = value


def join_coupled(left, right):
    d_re, d_im = complex_mul(left[2], left[3], right[0], right[1])
    inv_re, inv_im = reciprocal(1.0 - d_re, -d_im)
    f_re, f_im = complex_mul(left[4], left[5], right[0], right[1])
    f_re, f_im = complex_mul(f_re, f_im, inv_re, inv_im)
    g_re, g_im = complex_mul(right[4], right[5], left[2], left[3])
    g_re, g_im = complex_mul(g_re, g_im, inv_re, inv_im)
    x_re, x_im = complex_mul(left[4], left[5], right[4], right[5])
    x_re, x_im = complex_mul(x_re, x_im, inv_re, inv_im)
    x_re, x_im = complex_mul(x_re, x_im, inv_re, inv_im)
    return (left[0] + f_re, left[1] + f_im, right[2] + g_re, right[3] + g_im, x_re, x_im)


def in_order(refs, own, mixed):
    loaded = [ref[...] for ref in refs]
    if not mixed:
        return loaded
    ordered = []
    for position in range(len(refs)):
        offset = jnp.bitwise_xor(own, position)
        value = loaded[0]
        for index in range(1, len(refs)):
            value = jnp.where(offset == index, loaded[index], value)
        ordered.append(value)
    return ordered


def split_fields(value, points):
    return tuple(value[f * points:(f + 1) * points] for f in range(6))


def group_kernel(here_ref, *refs):
    local_refs, out_ref = refs[:-1], refs[-1]
    points = out_ref.shape[0] // 6
    size = len(local_refs)
    here = here_ref[0]
    blocks = in_order(local_refs, jnp.bitwise_and(here, size - 1), True)
    summary = split_fields(blocks[0], points)
    for member in range(1, size):
        summary = join_coupled(summary, split_fields(blocks[member], points))
    for index, value in enumerate(summary):
        out_ref[index * points:(index + 1) * points] = value


def final_kernel(here_ref, group_ref, length_ref, energy_ref, code_ref, *refs,
                 slots, points, devices, mixed, size, groups, scale):
    local_refs = refs[:size]
    group_refs = refs[size:size + groups]
    table_ref, dens_out_ref, bond_out_ref, theirs_ref, left_re_ref, left_im_ref, dens_ref, bond_ref = refs[size + groups:]
    here = here_ref[0]
    count = length_ref[here]
    rows = table_ref.shape[1]
    member_here = here % size
    group_here = here // size

    def into_step(block, run):
        run_re, run_im = run
        m_re, m_im = complex_mul(run_re, run_im, block[0], block[1])
        inv_re, inv_im = reciprocal(1.0 - m_re, -m_im)
        t_re, t_im = complex_mul(block[4], block[5], run_re, run_im)
        t_re, t_im = complex_mul(t_re, t_im, inv_re, inv_im)
        return (block[2] + t_re, block[3] + t_im)

    def from_step(block, run):
        run_re, run_im = run
        m_re, m_im = complex_mul(block[2], block[3], run_re, run_im)
        inv_re, inv_im = reciprocal(1.0 - m_re, -m_im)
        h_re, h_im = complex_mul(block[4], block[5], run_re, run_im)
        h_re, h_im = complex_mul(h_re, h_im, inv_re, inv_im)
        return (block[0] + h_re, block[1] + h_im)

    def masked(keep, new, old):
        return tuple(jnp.where(keep, n, o) for n, o in zip(new, old))

    zero = jnp.zeros((points,) + table_ref.shape[1:], jnp.float32)
    group_blocks = [split_fields(v, points) for v in in_order(group_refs, group_here, mixed)]
    local_blocks = [split_fields(v, points) for v in in_order(local_refs, member_here, mixed)]
    into = (zero, zero)
    for group in range(groups):
        into = masked(group < group_here, into_step(group_blocks[group], into), into)
    for member in range(size):
        into = masked(member < member_here, into_step(local_blocks[member], into), into)
    outof = (zero, zero)
    for group in reversed(range(groups)):
        outof = masked(group > group_here, from_step(group_blocks[group], outof), outof)
    for member in reversed(range(size)):
        outof = masked(member > member_here, from_step(local_blocks[member], outof), outof)
    into_re, into_im = into
    from_re, from_im = outof

    def onsite(slot):
        return onsite_terms(table_ref, energy_ref, here, count, devices, slots, points, slot)

    def forward_body(slot, carry):
        prev_re, prev_im, prev_coupling = carry
        onsite_re, onsite_im = onsite(slot)
        square = prev_coupling * prev_coupling
        g_re, g_im = reciprocal(onsite_re - square * prev_re, onsite_im - square * prev_im)
        left_re_ref[slot] = g_re
        left_im_ref[slot] = g_im
        return (g_re, g_im, table_ref[slots + slot])

    ones = jnp.ones(table_ref.shape[1:], jnp.float32)
    lax.fori_loop(0, count, forward_body, (into_re, into_im, ones))
    dens_ref[...] = jnp.zeros(dens_ref.shape, jnp.float32)
    bond_ref[...] = jnp.zeros(bond_ref.shape, jnp.float32)
    weights = [code_ref[point].astype(jnp.float32) * scale for point in range(points)]

    def backward_body(step, carry):
        next_re, next_im = carry
        slot = count - 1 - step
        onsite_re, onsite_im = onsite(slot)
        left_re, left_im = left_re_ref[slot], left_im_ref[slot]
        coupling = table_ref[slots + slot]
        square = coupling * coupling
        mix_re, mix_im = complex_mul(left_re, left_im, next_re, next_im)
        inv_re, inv_im = reciprocal(1.0 - square * mix_re, -square * mix_im)
        diag_re, diag_im = complex_mul(left_re, left_im, inv_re, inv_im)
        _, bond_im = complex_mul(diag_re, diag_im, next_re, next_im)
        dens = weights[0] * diag_im[0]
        bond = weights[0] * (square * bond_im[0])
        for point in range(1, points):
            dens = dens + weights[point] * diag_im[point]
            bond = bond + weights[point] * (square * bond_im[point])
        dens_ref[slot] = -inv_pi * dens
        bond_ref[slot] = -2.0 * inv_pi * bond
        return reciprocal(onsite_re - square * next_re, onsite_im - square * next_im)

    lax.fori_loop(0, count, backward_body, (from_re, from_im))
    lower = group_ref[0] == 0
    half = rows // 2
    for slot in range(slots):
        dens = dens_ref[slot]
        bond = bond_ref[slot]
        for row in range(half):
            lane = row * 128
            for kind, value, mine_ref in ((0, dens, dens_out_ref), (1, bond, bond_out_ref)):
                low, high = value[row:row + 1], value[row + half:row + half + 1]
                mine_ref[slot:slot + 1, lane:lane + 128] = jnp.where(lower, low, high)
                theirs_ref[kind, slot:slot + 1, lane:lane + 128] = jnp.where(lower, high, low)


def shards(
    mode_floor, onsite_noise, hopping, lengths, energy_index, weight_code, lead_shift, lead_width
):
    slots = onsite_noise.shape[0]
    modes = onsite_noise.shape[1]
    points = energy_index.shape[0]
    rows = modes // 128
    here = lax.axis_index("slab")
    devices = lax.axis_size("slab")
    groups = lax.axis_size("energy")
    table = jnp.concatenate(
        [
            mode_floor[None, :] + onsite_noise,
            hopping,
            lead_shift.reshape(2 * points, modes),
            lead_width.reshape(2 * points, modes),
        ],
        axis=0,
    ).reshape(2 * slots + 4 * points, rows, 128)
    here_arr = here.astype(jnp.int32).reshape(1)
    smem = pl.BlockSpec(memory_space=pltpu.SMEM)
    vmem = pl.BlockSpec(memory_space=pltpu.VMEM)

    packed = pl.pallas_call(
        functools.partial(summary_kernel, slots=slots, points=points, devices=devices),
        out_shape=jax.ShapeDtypeStruct((6 * points, rows, 128), jnp.float32),
        in_specs=[smem, smem, smem, vmem],
        out_specs=vmem,
    )(here_arr, lengths, energy_index, table)
    mixed = devices & (devices - 1) == 0 and devices >= 4
    if mixed:
        size = 4
        local = [packed] + [
            lax.ppermute(packed, "slab", [(device, device ^ offset) for device in range(devices)])
            for offset in range(1, size)
        ]
        summary = pl.pallas_call(
            group_kernel,
            out_shape=jax.ShapeDtypeStruct(packed.shape, jnp.float32),
            in_specs=[smem] + [vmem] * size,
            out_specs=vmem,
        )(here_arr, *local)
        if devices == size * size:
            every = [summary] + [
                lax.ppermute(summary, "slab", [(device, device ^ (offset * size)) for device in range(devices)])
                for offset in range(1, size)
            ]
        else:
            stacked = summary[None]
            distance = size
            while distance < devices:
                pairs = [(device, device ^ distance) for device in range(devices)]
                stacked = jnp.concatenate([stacked, lax.ppermute(stacked, "slab", pairs)], axis=0)
                distance *= 2
            every = [stacked[index] for index in range(devices // size)]
    else:
        size = devices
        gathered = lax.all_gather(packed, "slab")
        local = [gathered[index] for index in range(devices)]
        every = [jnp.zeros(packed.shape, jnp.float32)]
    half = jax.ShapeDtypeStruct((slots, modes // 2), jnp.float32)
    group_arr = lax.axis_index("energy").astype(jnp.int32).reshape(1)
    density, bond_density, theirs = pl.pallas_call(
        functools.partial(
            final_kernel, slots=slots, points=points, devices=devices, mixed=mixed,
            size=len(local), groups=len(every), scale=1.0 / (32.0 * points * groups),
        ),
        out_shape=(half, half, jax.ShapeDtypeStruct((2, slots, modes // 2), jnp.float32)),
        in_specs=[smem] * 5 + [vmem] * (len(local) + len(every) + 1),
        out_specs=(vmem, vmem, vmem),
        scratch_shapes=[
            pltpu.VMEM((slots, points, rows, 128), jnp.float32),
            pltpu.VMEM((slots, points, rows, 128), jnp.float32),
            pltpu.VMEM((slots, rows, 128), jnp.float32),
            pltpu.VMEM((slots, rows, 128), jnp.float32),
        ],
    )(here_arr, group_arr, lengths, energy_index, weight_code, *local, *every, table)
    if groups == 2:
        theirs = lax.ppermute(theirs, "energy", [(0, 1), (1, 0)])
        return (density + theirs[0], bond_density + theirs[1])
    lower = lax.axis_index("energy") == 0
    both = jnp.stack([
        jnp.where(lower, jnp.concatenate([density, theirs[0]], axis=1), jnp.concatenate([theirs[0], density], axis=1)),
        jnp.where(lower, jnp.concatenate([bond_density, theirs[1]], axis=1), jnp.concatenate([theirs[1], bond_density], axis=1)),
    ])
    both = lax.psum_scatter(both, "energy", scatter_dimension=2, tiled=True)
    return (both[0], both[1])


def solution(mesh):
    in_specs = (
        P(),
        P("slab", None),
        P("slab", None),
        P(),
        P("energy"),
        P("energy"),
        P("energy", None, None),
        P("energy", None, None),
    )
    out_specs = (P("slab", "energy"), P("slab", "energy"))
    return jax.shard_map(shards, mesh=mesh, in_specs=in_specs, out_specs=out_specs, check_vma=False)
```

profile of v0, /device:TPU:0, one launch (start us, length us, event | category | flops | bytes accessed | tf_op | source)
XLA Modules:
  0.0 39.4 jit_solution(9507702792215022751)
XLA Ops:
  0.6 0.0 copy-start.9
  0.6 0.0 copy-start.7
  0.7 0.8 %concatenate.14 = f32[8,8,128]{2,1,0:T(8,128)S(1)} reshape(f32[4,2,1024]{2,1,0:T(2,128)} %param.14) | data formatting | bytes 65536 | tf_op jit(solution)/shard_map/concatenate | solution.py:248
  1.5 0.0 copy-done.9
  1.5 0.0 copy-start.10
  1.5 0.0 copy-done.7
  1.5 0.6 %copy-done.10 = f32[1024]{0:T(1024)S(1)} copy-done((f32[1024]{0:T(1024)S(1)}, f32[1024]{0:T(1024)}, u32[]{:S(2)}) %copy-start.10) | copy-done | bytes 4120
  2.2 0.8 %copy-done.8 = f32[16,1024]{1,0:T(8,128)S(1)} copy-done((f32[16,1024]{1,0:T(8,128)S(1)}, f32[16,1024]{1,0:T(8,128)}, u32[]{:S(2)}) %copy-start.8) | copy-done | bytes 65560
  3.1 0.0 copy-start
  3.1 0.7 %copy-done = f32[48,8,128]{2,1,0:T(8,128)} copy-done((f32[48,8,128]{2,1,0:T(8,128)}, f32[48,8,128]{2,1,0:T(8,128)S(1)}, u32[]{:S(2)}) %copy-start) | copy-done | bytes 196632
  3.8 2.3 %shard_map.95.refs_0_ = f32[24,8,128]{2,1,0:T(8,128)} custom-call(s32[1]{0:T(128)} %bitcast.here_ref, s32[16]{0:T(128)} %length_ref.3, s32[4]{0:T(128)} %energy_ref.3, f32[48,8,128]{2,1,0:T(8,128)} %copy-done), custom_call_target="tpu_custom_call" | custom-call | tf_op jit(solution)/shard_map/pallas_call | solution.py:261
  6.0 2.0 %collective-permute-start.2 = (f32[24,8,128]{2,1,0:T(8,128)}, f32[24,8,128]{2,1,0:T(8,128)S(1)}, u32[]{:S(2)}, u32[]{:S(2)}) collective-permute-start(f32[24,8,128]{2,1,0:T(8,128)} %shard_map.95.refs_0_), channel_id=1, source_target_pairs={{0,6},{2,4},{4,2},{6,0},{8,14},{10,12},{12,10},{14,8},{16,22},{18,... | collective-permute-start | bytes 294920 | tf_op jit(solution)/shard_map/ppermute | solution.py:271
  8.0 1.3 %collective-permute-start.1 = (f32[24,8,128]{2,1,0:T(8,128)}, f32[24,8,128]{2,1,0:T(8,128)S(1)}, u32[]{:S(2)}, u32[]{:S(2)}) collective-permute-start(f32[24,8,128]{2,1,0:T(8,128)} %shard_map.95.refs_0_), channel_id=1, source_target_pairs={{0,4},{2,6},{4,0},{6,2},{8,12},{10,14},{12,8},{14,10},{16,20},{18,... | collective-permute-start | bytes 294920 | tf_op jit(solution)/shard_map/ppermute | solution.py:271
  9.3 0.1 collective-permute-start
  9.3 1.6 %collective-permute-done.2.refs_3_ = f32[24,8,128]{2,1,0:T(8,128)S(1)} collective-permute-done((f32[24,8,128]{2,1,0:T(8,128)}, f32[24,8,128]{2,1,0:T(8,128)S(1)}, u32[]{:S(2)}, u32[]{:S(2)}) %collective-permute-start.2) | collective-permute-done | bytes 98336 | tf_op jit(solution)/shard_map/ppermute | solution.py:271
  10.9 3.1 %collective-permute-done.1.refs_2_ = f32[24,8,128]{2,1,0:T(8,128)S(1)} collective-permute-done((f32[24,8,128]{2,1,0:T(8,128)}, f32[24,8,128]{2,1,0:T(8,128)S(1)}, u32[]{:S(2)}, u32[]{:S(2)}) %collective-permute-start.1) | collective-permute-done | bytes 98336 | tf_op jit(solution)/shard_map/ppermute | solution.py:271
  14.0 0.0 collective-permute-done.refs_1_
  14.0 0.6 %copy-done.2 = f32[24,8,128]{2,1,0:T(8,128)} copy-done((f32[24,8,128]{2,1,0:T(8,128)}, f32[24,8,128]{2,1,0:T(8,128)S(1)}, u32[]{:S(2)}) %copy-start.2) | copy-done | bytes 98328
  14.6 0.6 %copy-done.3 = f32[24,8,128]{2,1,0:T(8,128)} copy-done((f32[24,8,128]{2,1,0:T(8,128)}, f32[24,8,128]{2,1,0:T(8,128)S(1)}, u32[]{:S(2)}) %copy-start.3) | copy-done | bytes 98328
  15.3 1.8 %shard_map.96.refs_4_ = f32[24,8,128]{2,1,0:T(8,128)} custom-call(s32[1]{0:T(128)} %bitcast.here_ref, f32[24,8,128]{2,1,0:T(8,128)} %shard_map.95.refs_0_, f32[24,8,128]{2,1,0:T(8,128)} %copy-done.3, f32[24,8,128]{2,1,0:T(8,128)} %copy-done.2, f32[24,8,128]{2,1,0:T(8,128)} %copy-done.1), custom_call_target="tpu_custom_call" | custom-call | tf_op jit(solution)/shard_map/pallas_call | solution.py:274
  17.1 3.7 %collective-permute-start.5 = (f32[24,8,128]{2,1,0:T(8,128)}, f32[24,8,128]{2,1,0:T(8,128)S(1)}, u32[]{:S(2)}, u32[]{:S(2)}) collective-permute-start(f32[24,8,128]{2,1,0:T(8,128)} %shard_map.96.refs_4_), channel_id=1, source_target_pairs={{0,24},{2,26},{4,28},{6,30},{8,16},{10,18},{12,20},{14,22},{16,8},... | collective-permute-start | bytes 294920 | tf_op jit(solution)/shard_map/ppermute | solution.py:282
  20.8 0.0 collective-permute-start.4
  20.8 0.7 %collective-permute-start.3 = (f32[24,8,128]{2,1,0:T(8,128)}, f32[24,8,128]{2,1,0:T(8,128)S(1)}, u32[]{:S(2)}, u32[]{:S(2)}) collective-permute-start(f32[24,8,128]{2,1,0:T(8,128)} %shard_map.96.refs_4_), channel_id=1, source_target_pairs={{0,8},{2,10},{4,12},{6,14},{8,0},{10,2},{12,4},{14,6},{16,24},{18,... | collective-permute-start | bytes 294920 | tf_op jit(solution)/shard_map/ppermute | solution.py:282
  21.5 3.3 %collective-permute-done.5.refs_7_ = f32[24,8,128]{2,1,0:T(8,128)S(1)} collective-permute-done((f32[24,8,128]{2,1,0:T(8,128)}, f32[24,8,128]{2,1,0:T(8,128)S(1)}, u32[]{:S(2)}, u32[]{:S(2)}) %collective-permute-start.5) | collective-permute-done | bytes 98336 | tf_op jit(solution)/shard_map/ppermute | solution.py:282
  24.8 4.8 %collective-permute-done.4.refs_6_ = f32[24,8,128]{2,1,0:T(8,128)S(1)} collective-permute-done((f32[24,8,128]{2,1,0:T(8,128)}, f32[24,8,128]{2,1,0:T(8,128)S(1)}, u32[]{:S(2)}, u32[]{:S(2)}) %collective-permute-start.4) | collective-permute-done | bytes 98336 | tf_op jit(solution)/shard_map/ppermute | solution.py:282
  29.6 0.0 collective-permute-done.3.refs_5_
  29.6 0.6 %copy-done.5 = f32[24,8,128]{2,1,0:T(8,128)} copy-done((f32[24,8,128]{2,1,0:T(8,128)}, f32[24,8,128]{2,1,0:T(8,128)S(1)}, u32[]{:S(2)}) %copy-start.5) | copy-done | bytes 98328
  30.2 0.0 copy-done.6
  30.2 3.2 %shard_map.97 = (f32[16,512]{1,0:T(8,128)}, f32[16,512]{1,0:T(8,128)}, f32[2,16,512]{2,1,0:T(8,128)}) custom-call(s32[1]{0:T(128)} %bitcast.here_ref, s32[1]{0:T(128)} %bitcast.1.group_ref, s32[16]{0:T(128)} %length_ref.3, s32[4]{0:T(128)} %energy_ref.3, s32[4]{0:T(128)} %code_ref.1, f32[24,8,128]{2,1,0:T(8,128)} %shard_map.95.refs_0_, ...), custom_call_target="tpu_custom_call" | custom-call | tf_op jit(solution)/shard_map/pallas_call | solution.py:300
  33.5 1.7 %collective-permute-start.6 = (f32[2,16,512]{2,1,0:T(8,128)}, f32[2,16,512]{2,1,0:T(8,128)S(1)}, u32[]{:S(2)}, u32[]{:S(2)}) collective-permute-start(f32[2,16,512]{2,1,0:T(8,128)} %get-tuple-element.6), channel_id=1, source_target_pairs={{0,1},{1,0},{2,3},{3,2},{4,5},{5,4},{6,7},{7,6},{8,9},{9,8},{10,11... | collective-permute-start | bytes 196616 | tf_op jit(solution)/shard_map/ppermute | solution.py:316
  35.1 2.8 %collective-permute-done.6 = f32[2,16,512]{2,1,0:T(8,128)S(1)} collective-permute-done((f32[2,16,512]{2,1,0:T(8,128)}, f32[2,16,512]{2,1,0:T(8,128)S(1)}, u32[]{:S(2)}, u32[]{:S(2)}) %collective-permute-start.6) | collective-permute-done | bytes 65568 | tf_op jit(solution)/shard_map/ppermute | solution.py:316
  37.9 1.4 %fusion = (f32[16,512]{1,0:T(8,128)}, f32[16,512]{1,0:T(8,128)}) fusion(f32[16,512]{1,0:T(8,128)} %get-tuple-element.7, f32[2,16,512]{2,1,0:T(8,128)S(1)} %collective-permute-done.6, f32[16,512]{1,0:T(8,128)} %get-tuple-element.5), kind=kLoop, calls=%fused_computation.2 | loop fusion | flops 16384 | bytes 196608 | tf_op jit(solution)/shard_map/add | solution.py:317
  (17 shorter events, 0.1 us)
Async XLA Ops:
  0.6 0.8 %copy-start.9 = (f32[4,2,1024]{2,1,0:T(2,128)S(1)}, f32[4,2,1024]{2,1,0:T(2,128)}, u32[]{:S(2)}) copy-start(f32[4,2,1024]{2,1,0:T(2,128)} %param.15) | copy-start | bytes 98308
  0.6 0.9 %copy-start.7 = (f32[16,1024]{1,0:T(8,128)S(1)}, f32[16,1024]{1,0:T(8,128)}, u32[]{:S(2)}) copy-start(f32[16,1024]{1,0:T(8,128)} %param.9) | copy-start | bytes 196612
  1.5 0.7 %copy-start.10 = (f32[1024]{0:T(1024)S(1)}, f32[1024]{0:T(1024)}, u32[]{:S(2)}) copy-start(f32[1024]{0:T(1024)} %param.8) | copy-start | bytes 12292
  2.2 0.8 %copy-start.8 = (f32[16,1024]{1,0:T(8,128)S(1)}, f32[16,1024]{1,0:T(8,128)}, u32[]{:S(2)}) copy-start(f32[16,1024]{1,0:T(8,128)} %param.10) | copy-start | bytes 196612
  3.1 0.7 %copy-start = (f32[48,8,128]{2,1,0:T(8,128)}, f32[48,8,128]{2,1,0:T(8,128)S(1)}, u32[]{:S(2)}) copy-start(f32[48,8,128]{2,1,0:T(8,128)S(1)} %constant_dynamic-update-slice_fusion.table_ref.refs_8_) | copy-start | bytes 589828
  6.0 4.9 %collective-permute-start.2 = (f32[24,8,128]{2,1,0:T(8,128)}, f32[24,8,128]{2,1,0:T(8,128)S(1)}, u32[]{:S(2)}, u32[]{:S(2)}) collective-permute-start(f32[24,8,128]{2,1,0:T(8,128)} %shard_map.95.refs_0_), channel_id=1, source_target_pairs={{0,6},{2,4},{4,2},{6,0},{8,14},{10,12},{12,10},{14,8},{16,22},{18,... | collective-permute-start | bytes 294920 | tf_op jit(solution)/shard_map/ppermute | solution.py:271
  8.0 6.0 %collective-permute-start.1 = (f32[24,8,128]{2,1,0:T(8,128)}, f32[24,8,128]{2,1,0:T(8,128)S(1)}, u32[]{:S(2)}, u32[]{:S(2)}) collective-permute-start(f32[24,8,128]{2,1,0:T(8,128)} %shard_map.95.refs_0_), channel_id=1, source_target_pairs={{0,4},{2,6},{4,0},{6,2},{8,12},{10,14},{12,8},{14,10},{16,20},{18,... | collective-permute-start | bytes 294920 | tf_op jit(solution)/shard_map/ppermute | solution.py:271
  9.3 4.7 %collective-permute-start = (f32[24,8,128]{2,1,0:T(8,128)}, f32[24,8,128]{2,1,0:T(8,128)S(1)}, u32[]{:S(2)}, u32[]{:S(2)}) collective-permute-start(f32[24,8,128]{2,1,0:T(8,128)} %shard_map.95.refs_0_), channel_id=1, source_target_pairs={{0,2},{2,0},{4,6},{6,4},{8,10},{10,8},{12,14},{14,12},{16,18},{18,... | collective-permute-start | bytes 294920 | tf_op jit(solution)/shard_map/ppermute | solution.py:271
  10.9 3.1 %copy-start.1 = (f32[24,8,128]{2,1,0:T(8,128)}, f32[24,8,128]{2,1,0:T(8,128)S(1)}, u32[]{:S(2)}) copy-start(f32[24,8,128]{2,1,0:T(8,128)S(1)} %collective-permute-done.2.refs_3_) | copy-start | bytes 294916
  14.0 0.6 %copy-start.2 = (f32[24,8,128]{2,1,0:T(8,128)}, f32[24,8,128]{2,1,0:T(8,128)S(1)}, u32[]{:S(2)}) copy-start(f32[24,8,128]{2,1,0:T(8,128)S(1)} %collective-permute-done.1.refs_2_) | copy-start | bytes 294916
  14.6 0.6 %copy-start.3 = (f32[24,8,128]{2,1,0:T(8,128)}, f32[24,8,128]{2,1,0:T(8,128)S(1)}, u32[]{:S(2)}) copy-start(f32[24,8,128]{2,1,0:T(8,128)S(1)} %collective-permute-done.refs_1_) | copy-start | bytes 294916
  17.1 7.7 %collective-permute-start.5 = (f32[24,8,128]{2,1,0:T(8,128)}, f32[24,8,128]{2,1,0:T(8,128)S(1)}, u32[]{:S(2)}, u32[]{:S(2)}) collective-permute-start(f32[24,8,128]{2,1,0:T(8,128)} %shard_map.96.refs_4_), channel_id=1, source_target_pairs={{0,24},{2,26},{4,28},{6,30},{8,16},{10,18},{12,20},{14,22},{16,8},... | collective-permute-start | bytes 294920 | tf_op jit(solution)/shard_map/ppermute | solution.py:282
  20.8 8.8 %collective-permute-start.4 = (f32[24,8,128]{2,1,0:T(8,128)}, f32[24,8,128]{2,1,0:T(8,128)S(1)}, u32[]{:S(2)}, u32[]{:S(2)}) collective-permute-start(f32[24,8,128]{2,1,0:T(8,128)} %shard_map.96.refs_4_), channel_id=1, source_target_pairs={{0,16},{2,18},{4,20},{6,22},{8,24},{10,26},{12,28},{14,30},{16,0},... | collective-permute-start | bytes 294920 | tf_op jit(solution)/shard_map/ppermute | solution.py:282
  20.8 8.8 %collective-permute-start.3 = (f32[24,8,128]{2,1,0:T(8,128)}, f32[24,8,128]{2,1,0:T(8,128)S(1)}, u32[]{:S(2)}, u32[]{:S(2)}) collective-permute-start(f32[24,8,128]{2,1,0:T(8,128)} %shard_map.96.refs_4_), channel_id=1, source_target_pairs={{0,8},{2,10},{4,12},{6,14},{8,0},{10,2},{12,4},{14,6},{16,24},{18,... | collective-permute-start | bytes 294920 | tf_op jit(solution)/shard_map/ppermute | solution.py:282
  24.8 4.8 %copy-start.4 = (f32[24,8,128]{2,1,0:T(8,128)}, f32[24,8,128]{2,1,0:T(8,128)S(1)}, u32[]{:S(2)}) copy-start(f32[24,8,128]{2,1,0:T(8,128)S(1)} %collective-permute-done.5.refs_7_) | copy-start | bytes 294916
  29.6 0.6 %copy-start.5 = (f32[24,8,128]{2,1,0:T(8,128)}, f32[24,8,128]{2,1,0:T(8,128)S(1)}, u32[]{:S(2)}) copy-start(f32[24,8,128]{2,1,0:T(8,128)S(1)} %collective-permute-done.4.refs_6_) | copy-start | bytes 294916
  29.6 0.7 %copy-start.6 = (f32[24,8,128]{2,1,0:T(8,128)}, f32[24,8,128]{2,1,0:T(8,128)S(1)}, u32[]{:S(2)}) copy-start(f32[24,8,128]{2,1,0:T(8,128)S(1)} %collective-permute-done.3.refs_5_) | copy-start | bytes 294916
  33.5 4.5 %collective-permute-start.6 = (f32[2,16,512]{2,1,0:T(8,128)}, f32[2,16,512]{2,1,0:T(8,128)S(1)}, u32[]{:S(2)}, u32[]{:S(2)}) collective-permute-start(f32[2,16,512]{2,1,0:T(8,128)} %get-tuple-element.6), channel_id=1, source_target_pairs={{0,1},{1,0},{2,3},{3,2},{4,5},{5,4},{6,7},{7,6},{8,9},{9,8},{10,11... | collective-permute-start | bytes 196616 | tf_op jit(solution)/shard_map/ppermute | solution.py:316
where the time goes:
time: 40 us; the launch traced here: 39.4 us
  waiting for transfers between devices  15.6 us (39%)
  starting transfers between devices  9.35 us (23%)
  Pallas kernels  7.32 us (18%)
  local copies, waits for them, and re-layouts  4.93 us (12%)
  other arithmetic  1.42 us (4%)
  between operations  0.76 us (2%)
    ppermute x3, waiting for transfers between devices, shards(): lax.ppermute(summary, 'slab', [(device, device ^ offset * size) for devic...  8.11 us
    ppermute x3, waiting for transfers between devices, shards(): lax.ppermute(packed, 'slab', [(device, device ^ offset) for device in ran...  4.65 us
    ppermute x3, starting transfers between devices, shards(): lax.ppermute(summary, 'slab', [(device, device ^ offset * size) for devic...  4.39 us
    unnamed x27, local copies, waits for them, and re-layouts  4.08 us
    ppermute x3, starting transfers between devices, shards(): lax.ppermute(packed, 'slab', [(device, device ^ offset) for device in ran...  3.3 us
    pallas_call x1, Pallas kernels, shards(): pl.pallas_call(functools.partial(final_kernel, slots=slots, points=points...  3.21 us
    ppermute x1, waiting for transfers between devices, shards(): theirs = lax.ppermute(theirs, 'energy', [(0, 1), (1, 0)])  2.81 us
    pallas_call x1, Pallas kernels, shards(): pl.pallas_call(functools.partial(summary_kernel, slots=slots, points=poin...  2.28 us
  transfers between devices with their start and end apart: 7, of which 5 were waited for; matrix products, arithmetic and copies ran while one was open for 0% of the time, Pallas kernels for 0%

commit v1 on v0

--- a/solution.py
+++ b/solution.py
@@ -78,18 +78,16 @@
             table_ref, energy_ref, here, count, devices, slots, points, slot
         )
         g_re, g_im = reciprocal(onsite_re, onsite_im)
-        return (g_re, g_im, g_re, g_im, g_re, g_im, table_ref[slots + slot])
+        coupling = table_ref[slots + slot]
+        square = coupling * coupling
+        sq_re, sq_im = complex_mul(g_re, g_im, g_re, g_im)
+        return (g_re, g_im, square * g_re, square * g_im, square * sq_re, square * sq_im)
 
     def body(slot, summary):
-        return join_segments(summary, single(slot))
-
-    first_re, first_im, cross_re, cross_im, final_re, final_im, coupling = lax.fori_loop(
-        1, count, body, single(0)
-    )
-    square = coupling * coupling
-    sq_re, sq_im = complex_mul(cross_re, cross_im, cross_re, cross_im)
-    fields = (first_re, first_im, square * final_re, square * final_im, square * sq_re, square * sq_im)
-    for index, value in enumerate(fields):
+        return join_coupled(summary, single(slot))
+
+    summary = lax.fori_loop(1, count, body, single(0))
+    for index, value in enumerate(summary):
         out_ref[index * points:(index + 1) * points] = value
 
 

time: 40 us -> 39.8 us (level)
  Pallas kernels: 7.32 us -> 6.43 us
  starting transfers between devices: 9.35 us -> 10.1 us
    ppermute x3, starting transfers between devices: 4.39 us -> 5.58 us  [shards(): lax.ppermute(summary, 'slab', [(device, device ^ offset * size) for devic...]
    ppermute x3, waiting for transfers between devices: 8.11 us -> 7.33 us  [shards(): lax.ppermute(summary, 'slab', [(device, device ^ offset * size) for devic...]
    ppermute x1, waiting for transfers between devices: 2.81 us -> 3.28 us  [shards(): theirs = lax.ppermute(theirs, 'energy', [(0, 1), (1, 0)])]
    pallas_call x1, Pallas kernels: 3.21 us -> 2.75 us  [shards(): pl.pallas_call(functools.partial(final_kernel, slots=slots, points=points...]
    ppermute x3, waiting for transfers between devices: 4.65 us -> 5.11 us  [shards(): lax.ppermute(packed, 'slab', [(device, device ^ offset) for device in ran...]
    pallas_call x1, Pallas kernels: 2.28 us -> 1.85 us  [shards(): pl.pallas_call(functools.partial(summary_kernel, slots=slots, points=poin...]
where the time goes in v1:
time: 39.8 us; the launch traced here: 39.4 us
  waiting for transfers between devices  15.7 us (39%)
  starting transfers between devices  10.1 us (25%)
  Pallas kernels  6.43 us (16%)
  local copies, waits for them, and re-layouts  4.93 us (12%)
  other arithmetic  1.42 us (4%)
  between operations  0.76 us (2%)
    ppermute x3, waiting for transfers between devices, shards(): lax.ppermute(summary, 'slab', [(device, device ^ offset * size) for devic...  7.33 us
    ppermute x3, starting transfers between devices, shards(): lax.ppermute(summary, 'slab', [(device, device ^ offset * size) for devic...  5.58 us
    ppermute x3, waiting for transfers between devices, shards(): lax.ppermute(packed, 'slab', [(device, device ^ offset) for device in ran...  5.11 us
    unnamed x27, local copies, waits for them, and re-layouts  4.08 us
    ppermute x1, waiting for transfers between devices, shards(): theirs = lax.ppermute(theirs, 'energy', [(0, 1), (1, 0)])  3.28 us
    ppermute x3, starting transfers between devices, shards(): lax.ppermute(packed, 'slab', [(device, device ^ offset) for device in ran...  3 us
    pallas_call x1, Pallas kernels, shards(): pl.pallas_call(functools.partial(final_kernel, slots=slots, points=points...  2.75 us
    pallas_call x1, Pallas kernels, shards(): pl.pallas_call(functools.partial(summary_kernel, slots=slots, points=poin...  1.85 us
  transfers between devices with their start and end apart: 7, of which 5 were waited for; matrix products, arithmetic and copies ran while one was open for 0% of the time, Pallas kernels for 0%

profile of v1, /device:TPU:0, one launch (start us, length us, event | category | flops | bytes accessed | tf_op | source)
XLA Modules:
  0.0 39.4 jit_solution(2417867681008674072)
XLA Ops:
  0.6 0.0 copy-start.9
  0.6 0.0 copy-start.7
  0.7 0.8 %concatenate.14 = f32[8,8,128]{2,1,0:T(8,128)S(1)} reshape(f32[4,2,1024]{2,1,0:T(2,128)} %param.14) | data formatting | bytes 65536 | tf_op jit(solution)/shard_map/concatenate | solution.py:246
  1.5 0.0 copy-done.9
  1.5 0.0 copy-start.10
  1.5 0.6 %copy-done.10 = f32[1024]{0:T(1024)S(1)} copy-done((f32[1024]{0:T(1024)S(1)}, f32[1024]{0:T(1024)}, u32[]{:S(2)}) %copy-start.10) | copy-done | bytes 4120
  2.2 0.8 %copy-done.8 = f32[16,1024]{1,0:T(8,128)S(1)} copy-done((f32[16,1024]{1,0:T(8,128)S(1)}, f32[16,1024]{1,0:T(8,128)}, u32[]{:S(2)}) %copy-start.8) | copy-done | bytes 65560
  3.1 0.0 copy-start
  3.1 0.7 %copy-done = f32[48,8,128]{2,1,0:T(8,128)} copy-done((f32[48,8,128]{2,1,0:T(8,128)}, f32[48,8,128]{2,1,0:T(8,128)S(1)}, u32[]{:S(2)}) %copy-start) | copy-done | bytes 196632
  3.8 1.9 %shard_map.95.refs_0_ = f32[24,8,128]{2,1,0:T(8,128)} custom-call(s32[1]{0:T(128)} %bitcast.here_ref, s32[16]{0:T(128)} %length_ref.3, s32[4]{0:T(128)} %energy_ref.3, f32[48,8,128]{2,1,0:T(8,128)} %copy-done), custom_call_target="tpu_custom_call" | custom-call | tf_op jit(solution)/shard_map/pallas_call | solution.py:259
  5.6 2.4 %collective-permute-start.2 = (f32[24,8,128]{2,1,0:T(8,128)}, f32[24,8,128]{2,1,0:T(8,128)S(1)}, u32[]{:S(2)}, u32[]{:S(2)}) collective-permute-start(f32[24,8,128]{2,1,0:T(8,128)} %shard_map.95.refs_0_), channel_id=1, source_target_pairs={{0,6},{2,4},{4,2},{6,0},{8,14},{10,12},{12,10},{14,8},{16,22},{18,... | collective-permute-start | bytes 294920 | tf_op jit(solution)/shard_map/ppermute | solution.py:269
  8.1 0.5 %collective-permute-start.1 = (f32[24,8,128]{2,1,0:T(8,128)}, f32[24,8,128]{2,1,0:T(8,128)S(1)}, u32[]{:S(2)}, u32[]{:S(2)}) collective-permute-start(f32[24,8,128]{2,1,0:T(8,128)} %shard_map.95.refs_0_), channel_id=1, source_target_pairs={{0,4},{2,6},{4,0},{6,2},{8,12},{10,14},{12,8},{14,10},{16,20},{18,... | collective-permute-start | bytes 294920 | tf_op jit(solution)/shard_map/ppermute | solution.py:269
  8.5 0.1 collective-permute-start
  8.6 2.9 %collective-permute-done.2.refs_3_ = f32[24,8,128]{2,1,0:T(8,128)S(1)} collective-permute-done((f32[24,8,128]{2,1,0:T(8,128)}, f32[24,8,128]{2,1,0:T(8,128)S(1)}, u32[]{:S(2)}, u32[]{:S(2)}) %collective-permute-start.2) | collective-permute-done | bytes 98336 | tf_op jit(solution)/shard_map/ppermute | solution.py:269
  11.6 2.2 %collective-permute-done.1.refs_2_ = f32[24,8,128]{2,1,0:T(8,128)S(1)} collective-permute-done((f32[24,8,128]{2,1,0:T(8,128)}, f32[24,8,128]{2,1,0:T(8,128)S(1)}, u32[]{:S(2)}, u32[]{:S(2)}) %collective-permute-start.1) | collective-permute-done | bytes 98336 | tf_op jit(solution)/shard_map/ppermute | solution.py:269
  13.7 0.0 collective-permute-done.refs_1_
  13.7 0.0 copy-done.1
  13.7 0.6 %copy-done.2 = f32[24,8,128]{2,1,0:T(8,128)} copy-done((f32[24,8,128]{2,1,0:T(8,128)}, f32[24,8,128]{2,1,0:T(8,128)S(1)}, u32[]{:S(2)}) %copy-start.2) | copy-done | bytes 98328
  14.4 0.6 %copy-done.3 = f32[24,8,128]{2,1,0:T(8,128)} copy-done((f32[24,8,128]{2,1,0:T(8,128)}, f32[24,8,128]{2,1,0:T(8,128)S(1)}, u32[]{:S(2)}) %copy-start.3) | copy-done | bytes 98328
  15.0 1.8 %shard_map.96.refs_4_ = f32[24,8,128]{2,1,0:T(8,128)} custom-call(s32[1]{0:T(128)} %bitcast.here_ref, f32[24,8,128]{2,1,0:T(8,128)} %shard_map.95.refs_0_, f32[24,8,128]{2,1,0:T(8,128)} %copy-done.3, f32[24,8,128]{2,1,0:T(8,128)} %copy-done.2, f32[24,8,128]{2,1,0:T(8,128)} %copy-done.1), custom_call_target="tpu_custom_call" | custom-call | tf_op jit(solution)/shard_map/pallas_call | solution.py:272
  16.8 5.0 %collective-permute-start.5 = (f32[24,8,128]{2,1,0:T(8,128)}, f32[24,8,128]{2,1,0:T(8,128)S(1)}, u32[]{:S(2)}, u32[]{:S(2)}) collective-permute-start(f32[24,8,128]{2,1,0:T(8,128)} %shard_map.96.refs_4_), channel_id=1, source_target_pairs={{0,24},{2,26},{4,28},{6,30},{8,16},{10,18},{12,20},{14,22},{16,8},... | collective-permute-start | bytes 294920 | tf_op jit(solution)/shard_map/ppermute | solution.py:280
  21.8 0.0 collective-permute-start.4
  21.8 0.6 %collective-permute-start.3 = (f32[24,8,128]{2,1,0:T(8,128)}, f32[24,8,128]{2,1,0:T(8,128)S(1)}, u32[]{:S(2)}, u32[]{:S(2)}) collective-permute-start(f32[24,8,128]{2,1,0:T(8,128)} %shard_map.96.refs_4_), channel_id=1, source_target_pairs={{0,8},{2,10},{4,12},{6,14},{8,0},{10,2},{12,4},{14,6},{16,24},{18,... | collective-permute-start | bytes 294920 | tf_op jit(solution)/shard_map/ppermute | solution.py:280
  22.4 3.3 %collective-permute-done.5.refs_7_ = f32[24,8,128]{2,1,0:T(8,128)S(1)} collective-permute-done((f32[24,8,128]{2,1,0:T(8,128)}, f32[24,8,128]{2,1,0:T(8,128)S(1)}, u32[]{:S(2)}, u32[]{:S(2)}) %collective-permute-start.5) | collective-permute-done | bytes 98336 | tf_op jit(solution)/shard_map/ppermute | solution.py:280
  25.7 4.0 %collective-permute-done.4.refs_6_ = f32[24,8,128]{2,1,0:T(8,128)S(1)} collective-permute-done((f32[24,8,128]{2,1,0:T(8,128)}, f32[24,8,128]{2,1,0:T(8,128)S(1)}, u32[]{:S(2)}, u32[]{:S(2)}) %collective-permute-start.4) | collective-permute-done | bytes 98336 | tf_op jit(solution)/shard_map/ppermute | solution.py:280
  29.7 0.0 collective-permute-done.3.refs_5_
  29.7 0.6 %copy-done.5 = f32[24,8,128]{2,1,0:T(8,128)} copy-done((f32[24,8,128]{2,1,0:T(8,128)}, f32[24,8,128]{2,1,0:T(8,128)S(1)}, u32[]{:S(2)}) %copy-start.5) | copy-done | bytes 98328
  30.4 0.0 copy-done.6
  30.4 2.8 %shard_map.97 = (f32[16,512]{1,0:T(8,128)}, f32[16,512]{1,0:T(8,128)}, f32[2,16,512]{2,1,0:T(8,128)}) custom-call(s32[1]{0:T(128)} %bitcast.here_ref, s32[1]{0:T(128)} %bitcast.1.group_ref, s32[16]{0:T(128)} %length_ref.3, s32[4]{0:T(128)} %energy_ref.3, s32[4]{0:T(128)} %code_ref.1, f32[24,8,128]{2,1,0:T(8,128)} %shard_map.95.refs_0_, ...), custom_call_target="tpu_custom_call" | custom-call | tf_op jit(solution)/shard_map/pallas_call | solution.py:298
  33.1 1.5 %collective-permute-start.6 = (f32[2,16,512]{2,1,0:T(8,128)}, f32[2,16,512]{2,1,0:T(8,128)S(1)}, u32[]{:S(2)}, u32[]{:S(2)}) collective-permute-start(f32[2,16,512]{2,1,0:T(8,128)} %get-tuple-element.6), channel_id=1, source_target_pairs={{0,1},{1,0},{2,3},{3,2},{4,5},{5,4},{6,7},{7,6},{8,9},{9,8},{10,11... | collective-permute-start | bytes 196616 | tf_op jit(solution)/shard_map/ppermute | solution.py:314
  34.7 3.3 %collective-permute-done.6 = f32[2,16,512]{2,1,0:T(8,128)S(1)} collective-permute-done((f32[2,16,512]{2,1,0:T(8,128)}, f32[2,16,512]{2,1,0:T(8,128)S(1)}, u32[]{:S(2)}, u32[]{:S(2)}) %collective-permute-start.6) | collective-permute-done | bytes 65568 | tf_op jit(solution)/shard_map/ppermute | solution.py:314
  37.9 1.4 %fusion = (f32[16,512]{1,0:T(8,128)}, f32[16,512]{1,0:T(8,128)}) fusion(f32[16,512]{1,0:T(8,128)} %get-tuple-element.7, f32[2,16,512]{2,1,0:T(8,128)S(1)} %collective-permute-done.6, f32[16,512]{1,0:T(8,128)} %get-tuple-element.5), kind=kLoop, calls=%fused_computation.2 | loop fusion | flops 16384 | bytes 196608 | tf_op jit(solution)/shard_map/add | solution.py:315
  (17 shorter events, 0.1 us)
Async XLA Ops:
  0.6 0.8 %copy-start.9 = (f32[4,2,1024]{2,1,0:T(2,128)S(1)}, f32[4,2,1024]{2,1,0:T(2,128)}, u32[]{:S(2)}) copy-start(f32[4,2,1024]{2,1,0:T(2,128)} %param.15) | copy-start | bytes 98308
  0.6 0.9 %copy-start.7 = (f32[16,1024]{1,0:T(8,128)S(1)}, f32[16,1024]{1,0:T(8,128)}, u32[]{:S(2)}) copy-start(f32[16,1024]{1,0:T(8,128)} %param.9) | copy-start | bytes 196612
  1.5 0.7 %copy-start.10 = (f32[1024]{0:T(1024)S(1)}, f32[1024]{0:T(1024)}, u32[]{:S(2)}) copy-start(f32[1024]{0:T(1024)} %param.8) | copy-start | bytes 12292
  2.2 0.8 %copy-start.8 = (f32[16,1024]{1,0:T(8,128)S(1)}, f32[16,1024]{1,0:T(8,128)}, u32[]{:S(2)}) copy-start(f32[16,1024]{1,0:T(8,128)} %param.10) | copy-start | bytes 196612
  3.1 0.7 %copy-start = (f32[48,8,128]{2,1,0:T(8,128)}, f32[48,8,128]{2,1,0:T(8,128)S(1)}, u32[]{:S(2)}) copy-start(f32[48,8,128]{2,1,0:T(8,128)S(1)} %constant_dynamic-update-slice_fusion.table_ref.refs_8_) | copy-start | bytes 589828
  5.6 5.9 %collective-permute-start.2 = (f32[24,8,128]{2,1,0:T(8,128)}, f32[24,8,128]{2,1,0:T(8,128)S(1)}, u32[]{:S(2)}, u32[]{:S(2)}) collective-permute-start(f32[24,8,128]{2,1,0:T(8,128)} %shard_map.95.refs_0_), channel_id=1, source_target_pairs={{0,6},{2,4},{4,2},{6,0},{8,14},{10,12},{12,10},{14,8},{16,22},{18,... | collective-permute-start | bytes 294920 | tf_op jit(solution)/shard_map/ppermute | solution.py:269
  8.1 5.7 %collective-permute-start.1 = (f32[24,8,128]{2,1,0:T(8,128)}, f32[24,8,128]{2,1,0:T(8,128)S(1)}, u32[]{:S(2)}, u32[]{:S(2)}) collective-permute-start(f32[24,8,128]{2,1,0:T(8,128)} %shard_map.95.refs_0_), channel_id=1, source_target_pairs={{0,4},{2,6},{4,0},{6,2},{8,12},{10,14},{12,8},{14,10},{16,20},{18,... | collective-permute-start | bytes 294920 | tf_op jit(solution)/shard_map/ppermute | solution.py:269
  8.5 5.2 %collective-permute-start = (f32[24,8,128]{2,1,0:T(8,128)}, f32[24,8,128]{2,1,0:T(8,128)S(1)}, u32[]{:S(2)}, u32[]{:S(2)}) collective-permute-start(f32[24,8,128]{2,1,0:T(8,128)} %shard_map.95.refs_0_), channel_id=1, source_target_pairs={{0,2},{2,0},{4,6},{6,4},{8,10},{10,8},{12,14},{14,12},{16,18},{18,... | collective-permute-start | bytes 294920 | tf_op jit(solution)/shard_map/ppermute | solution.py:269
  11.6 2.2 %copy-start.1 = (f32[24,8,128]{2,1,0:T(8,128)}, f32[24,8,128]{2,1,0:T(8,128)S(1)}, u32[]{:S(2)}) copy-start(f32[24,8,128]{2,1,0:T(8,128)S(1)} %collective-permute-done.2.refs_3_) | copy-start | bytes 294916
  13.7 0.6 %copy-start.2 = (f32[24,8,128]{2,1,0:T(8,128)}, f32[24,8,128]{2,1,0:T(8,128)S(1)}, u32[]{:S(2)}) copy-start(f32[24,8,128]{2,1,0:T(8,128)S(1)} %collective-permute-done.1.refs_2_) | copy-start | bytes 294916
  14.4 0.6 %copy-start.3 = (f32[24,8,128]{2,1,0:T(8,128)}, f32[24,8,128]{2,1,0:T(8,128)S(1)}, u32[]{:S(2)}) copy-start(f32[24,8,128]{2,1,0:T(8,128)S(1)} %collective-permute-done.refs_1_) | copy-start | bytes 294916
  16.8 8.9 %collective-permute-start.5 = (f32[24,8,128]{2,1,0:T(8,128)}, f32[24,8,128]{2,1,0:T(8,128)S(1)}, u32[]{:S(2)}, u32[]{:S(2)}) collective-permute-start(f32[24,8,128]{2,1,0:T(8,128)} %shard_map.96.refs_4_), channel_id=1, source_target_pairs={{0,24},{2,26},{4,28},{6,30},{8,16},{10,18},{12,20},{14,22},{16,8},... | collective-permute-start | bytes 294920 | tf_op jit(solution)/shard_map/ppermute | solution.py:280
  21.8 7.9 %collective-permute-start.4 = (f32[24,8,128]{2,1,0:T(8,128)}, f32[24,8,128]{2,1,0:T(8,128)S(1)}, u32[]{:S(2)}, u32[]{:S(2)}) collective-permute-start(f32[24,8,128]{2,1,0:T(8,128)} %shard_map.96.refs_4_), channel_id=1, source_target_pairs={{0,16},{2,18},{4,20},{6,22},{8,24},{10,26},{12,28},{14,30},{16,0},... | collective-permute-start | bytes 294920 | tf_op jit(solution)/shard_map/ppermute | solution.py:280
  21.8 7.9 %collective-permute-start.3 = (f32[24,8,128]{2,1,0:T(8,128)}, f32[24,8,128]{2,1,0:T(8,128)S(1)}, u32[]{:S(2)}, u32[]{:S(2)}) collective-permute-start(f32[24,8,128]{2,1,0:T(8,128)} %shard_map.96.refs_4_), channel_id=1, source_target_pairs={{0,8},{2,10},{4,12},{6,14},{8,0},{10,2},{12,4},{14,6},{16,24},{18,... | collective-permute-start | bytes 294920 | tf_op jit(solution)/shard_map/ppermute | solution.py:280
  25.7 4.0 %copy-start.4 = (f32[24,8,128]{2,1,0:T(8,128)}, f32[24,8,128]{2,1,0:T(8,128)S(1)}, u32[]{:S(2)}) copy-start(f32[24,8,128]{2,1,0:T(8,128)S(1)} %collective-permute-done.5.refs_7_) | copy-start | bytes 294916
  29.7 0.6 %copy-start.5 = (f32[24,8,128]{2,1,0:T(8,128)}, f32[24,8,128]{2,1,0:T(8,128)S(1)}, u32[]{:S(2)}) copy-start(f32[24,8,128]{2,1,0:T(8,128)S(1)} %collective-permute-done.4.refs_6_) | copy-start | bytes 294916
  29.7 0.7 %copy-start.6 = (f32[24,8,128]{2,1,0:T(8,128)}, f32[24,8,128]{2,1,0:T(8,128)S(1)}, u32[]{:S(2)}) copy-start(f32[24,8,128]{2,1,0:T(8,128)S(1)} %collective-permute-done.3.refs_5_) | copy-start | bytes 294916
  33.1 4.8 %collective-permute-start.6 = (f32[2,16,512]{2,1,0:T(8,128)}, f32[2,16,512]{2,1,0:T(8,128)S(1)}, u32[]{:S(2)}, u32[]{:S(2)}) collective-permute-start(f32[2,16,512]{2,1,0:T(8,128)} %get-tuple-element.6), channel_id=1, source_target_pairs={{0,1},{1,0},{2,3},{3,2},{4,5},{5,4},{6,7},{7,6},{8,9},{9,8},{10,11... | collective-permute-start | bytes 196616 | tf_op jit(solution)/shard_map/ppermute | solution.py:314

commit v2 on v1

--- a/solution.py
+++ b/solution.py
@@ -188,9 +188,10 @@
         prev_re, prev_im, prev_coupling = carry
         onsite_re, onsite_im = onsite(slot)
         square = prev_coupling * prev_coupling
-        g_re, g_im = reciprocal(onsite_re - square * prev_re, onsite_im - square * prev_im)
-        left_re_ref[slot] = g_re
-        left_im_ref[slot] = g_im
+        denom_re, denom_im = onsite_re - square * prev_re, onsite_im - square * prev_im
+        g_re, g_im = reciprocal(denom_re, denom_im)
+        left_re_ref[slot] = denom_re
+        left_im_ref[slot] = denom_im
         return (g_re, g_im, table_ref[slots + slot])
 
     ones = jnp.ones(table_ref.shape[1:], jnp.float32)
@@ -203,12 +204,10 @@
         next_re, next_im = carry
         slot = count - 1 - step
         onsite_re, onsite_im = onsite(slot)
-        left_re, left_im = left_re_ref[slot], left_im_ref[slot]
+        denom_re, denom_im = left_re_ref[slot], left_im_ref[slot]
         coupling = table_ref[slots + slot]
         square = coupling * coupling
-        mix_re, mix_im = complex_mul(left_re, left_im, next_re, next_im)
-        inv_re, inv_im = reciprocal(1.0 - square * mix_re, -square * mix_im)
-        diag_re, diag_im = complex_mul(left_re, left_im, inv_re, inv_im)
+        diag_re, diag_im = reciprocal(denom_re - square * next_re, denom_im - square * next_im)
         _, bond_im = complex_mul(diag_re, diag_im, next_re, next_im)
         dens = weights[0] * diag_im[0]
         bond = weights[0] * (square * bond_im[0])

time: 39.8 us -> 39.8 us (level)
  starting transfers between devices: 10.1 us -> 8.72 us
  waiting for transfers between devices: 15.7 us -> 16.9 us
    ppermute x3, waiting for transfers between devices: 7.33 us -> 8.53 us  [shards(): lax.ppermute(summary, 'slab', [(device, device ^ offset * size) for devic...]
    ppermute x3, starting transfers between devices: 5.58 us -> 4.39 us  [shards(): lax.ppermute(summary, 'slab', [(device, device ^ offset * size) for devic...]
where the time goes in v2:
time: 39.8 us; the launch traced here: 39.4 us
  waiting for transfers between devices  16.9 us (42%)
  starting transfers between devices  8.72 us (22%)
  Pallas kernels  6.63 us (17%)
  local copies, waits for them, and re-layouts  4.93 us (12%)
  other arithmetic  1.42 us (4%)
  between operations  0.76 us (2%)
    ppermute x3, waiting for transfers between devices, shards(): lax.ppermute(summary, 'slab', [(device, device ^ offset * size) for devic...  8.53 us
    ppermute x3, waiting for transfers between devices, shards(): lax.ppermute(packed, 'slab', [(device, device ^ offset) for device in ran...  5.41 us
    ppermute x3, starting transfers between devices, shards(): lax.ppermute(summary, 'slab', [(device, device ^ offset * size) for devic...  4.39 us
    unnamed x27, local copies, waits for them, and re-layouts  4.08 us
    ppermute x1, waiting for transfers between devices, shards(): theirs = lax.ppermute(theirs, 'energy', [(0, 1), (1, 0)])  2.96 us
    pallas_call x1, Pallas kernels, shards(): pl.pallas_call(functools.partial(final_kernel, slots=slots, points=points...  2.82 us
    ppermute x3, starting transfers between devices, shards(): lax.ppermute(packed, 'slab', [(device, device ^ offset) for device in ran...  2.82 us
    pallas_call x1, Pallas kernels, shards(): pl.pallas_call(functools.partial(summary_kernel, slots=slots, points=poin...  1.97 us
  transfers between devices with their start and end apart: 7, of which 5 were waited for; matrix products, arithmetic and copies ran while one was open for 0% of the time, Pallas kernels for 0%

profile of v2, /device:TPU:0, one launch (start us, length us, event | category | flops | bytes accessed | tf_op | source)
XLA Modules:
  0.0 39.4 jit_solution(4733013505891615829)
XLA Ops:
  0.6 0.0 copy-start.9
  0.6 0.0 copy-start.7
  0.7 0.8 %concatenate.14 = f32[8,8,128]{2,1,0:T(8,128)S(1)} reshape(f32[4,2,1024]{2,1,0:T(2,128)} %param.14) | data formatting | bytes 65536 | tf_op jit(solution)/shard_map/concatenate | solution.py:245
  1.5 0.0 copy-done.9
  1.5 0.0 copy-start.10
  1.5 0.0 copy-done.7
  1.5 0.6 %copy-done.10 = f32[1024]{0:T(1024)S(1)} copy-done((f32[1024]{0:T(1024)S(1)}, f32[1024]{0:T(1024)}, u32[]{:S(2)}) %copy-start.10) | copy-done | bytes 4120
  2.2 0.8 %copy-done.8 = f32[16,1024]{1,0:T(8,128)S(1)} copy-done((f32[16,1024]{1,0:T(8,128)S(1)}, f32[16,1024]{1,0:T(8,128)}, u32[]{:S(2)}) %copy-start.8) | copy-done | bytes 65560
  3.1 0.7 %copy-done = f32[48,8,128]{2,1,0:T(8,128)} copy-done((f32[48,8,128]{2,1,0:T(8,128)}, f32[48,8,128]{2,1,0:T(8,128)S(1)}, u32[]{:S(2)}) %copy-start) | copy-done | bytes 196632
  3.8 2.0 %shard_map.95.refs_0_ = f32[24,8,128]{2,1,0:T(8,128)} custom-call(s32[1]{0:T(128)} %bitcast.here_ref, s32[16]{0:T(128)} %length_ref.3, s32[4]{0:T(128)} %energy_ref.3, f32[48,8,128]{2,1,0:T(8,128)} %copy-done), custom_call_target="tpu_custom_call" | custom-call | tf_op jit(solution)/shard_map/pallas_call | solution.py:258
  5.7 2.6 %collective-permute-start.2 = (f32[24,8,128]{2,1,0:T(8,128)}, f32[24,8,128]{2,1,0:T(8,128)S(1)}, u32[]{:S(2)}, u32[]{:S(2)}) collective-permute-start(f32[24,8,128]{2,1,0:T(8,128)} %shard_map.95.refs_0_), channel_id=1, source_target_pairs={{0,6},{2,4},{4,2},{6,0},{8,14},{10,12},{12,10},{14,8},{16,22},{18,... | collective-permute-start | bytes 294920 | tf_op jit(solution)/shard_map/ppermute | solution.py:268
  8.3 0.2 collective-permute-start.1
  8.5 0.1 collective-permute-start
  8.6 3.2 %collective-permute-done.2.refs_3_ = f32[24,8,128]{2,1,0:T(8,128)S(1)} collective-permute-done((f32[24,8,128]{2,1,0:T(8,128)}, f32[24,8,128]{2,1,0:T(8,128)S(1)}, u32[]{:S(2)}, u32[]{:S(2)}) %collective-permute-start.2) | collective-permute-done | bytes 98336 | tf_op jit(solution)/shard_map/ppermute | solution.py:268
  11.7 2.2 %collective-permute-done.1.refs_2_ = f32[24,8,128]{2,1,0:T(8,128)S(1)} collective-permute-done((f32[24,8,128]{2,1,0:T(8,128)}, f32[24,8,128]{2,1,0:T(8,128)S(1)}, u32[]{:S(2)}, u32[]{:S(2)}) %collective-permute-start.1) | collective-permute-done | bytes 98336 | tf_op jit(solution)/shard_map/ppermute | solution.py:268
  14.0 0.0 collective-permute-done.refs_1_
  14.0 0.0 copy-done.1
  14.0 0.6 %copy-done.2 = f32[24,8,128]{2,1,0:T(8,128)} copy-done((f32[24,8,128]{2,1,0:T(8,128)}, f32[24,8,128]{2,1,0:T(8,128)S(1)}, u32[]{:S(2)}) %copy-start.2) | copy-done | bytes 98328
  14.6 0.6 %copy-done.3 = f32[24,8,128]{2,1,0:T(8,128)} copy-done((f32[24,8,128]{2,1,0:T(8,128)}, f32[24,8,128]{2,1,0:T(8,128)S(1)}, u32[]{:S(2)}) %copy-start.3) | copy-done | bytes 98328
  15.2 1.8 %shard_map.96.refs_4_ = f32[24,8,128]{2,1,0:T(8,128)} custom-call(s32[1]{0:T(128)} %bitcast.here_ref, f32[24,8,128]{2,1,0:T(8,128)} %shard_map.95.refs_0_, f32[24,8,128]{2,1,0:T(8,128)} %copy-done.3, f32[24,8,128]{2,1,0:T(8,128)} %copy-done.2, f32[24,8,128]{2,1,0:T(8,128)} %copy-done.1), custom_call_target="tpu_custom_call" | custom-call | tf_op jit(solution)/shard_map/pallas_call | solution.py:271
  17.1 3.7 %collective-permute-start.5 = (f32[24,8,128]{2,1,0:T(8,128)}, f32[24,8,128]{2,1,0:T(8,128)S(1)}, u32[]{:S(2)}, u32[]{:S(2)}) collective-permute-start(f32[24,8,128]{2,1,0:T(8,128)} %shard_map.96.refs_4_), channel_id=1, source_target_pairs={{0,24},{2,26},{4,28},{6,30},{8,16},{10,18},{12,20},{14,22},{16,8},... | collective-permute-start | bytes 294920 | tf_op jit(solution)/shard_map/ppermute | solution.py:279
  20.8 0.0 collective-permute-start.4
  20.8 0.7 %collective-permute-start.3 = (f32[24,8,128]{2,1,0:T(8,128)}, f32[24,8,128]{2,1,0:T(8,128)S(1)}, u32[]{:S(2)}, u32[]{:S(2)}) collective-permute-start(f32[24,8,128]{2,1,0:T(8,128)} %shard_map.96.refs_4_), channel_id=1, source_target_pairs={{0,8},{2,10},{4,12},{6,14},{8,0},{10,2},{12,4},{14,6},{16,24},{18,... | collective-permute-start | bytes 294920 | tf_op jit(solution)/shard_map/ppermute | solution.py:279
  21.4 3.3 %collective-permute-done.5.refs_7_ = f32[24,8,128]{2,1,0:T(8,128)S(1)} collective-permute-done((f32[24,8,128]{2,1,0:T(8,128)}, f32[24,8,128]{2,1,0:T(8,128)S(1)}, u32[]{:S(2)}, u32[]{:S(2)}) %collective-permute-start.5) | collective-permute-done | bytes 98336 | tf_op jit(solution)/shard_map/ppermute | solution.py:279
  24.8 5.2 %collective-permute-done.4.refs_6_ = f32[24,8,128]{2,1,0:T(8,128)S(1)} collective-permute-done((f32[24,8,128]{2,1,0:T(8,128)}, f32[24,8,128]{2,1,0:T(8,128)S(1)}, u32[]{:S(2)}, u32[]{:S(2)}) %collective-permute-start.4) | collective-permute-done | bytes 98336 | tf_op jit(solution)/shard_map/ppermute | solution.py:279
  30.0 0.0 collective-permute-done.3.refs_5_
  30.0 0.6 %copy-done.5 = f32[24,8,128]{2,1,0:T(8,128)} copy-done((f32[24,8,128]{2,1,0:T(8,128)}, f32[24,8,128]{2,1,0:T(8,128)S(1)}, u32[]{:S(2)}) %copy-start.5) | copy-done | bytes 98328
  30.6 0.0 copy-done.6
  30.6 2.8 %shard_map.97 = (f32[16,512]{1,0:T(8,128)}, f32[16,512]{1,0:T(8,128)}, f32[2,16,512]{2,1,0:T(8,128)}) custom-call(s32[1]{0:T(128)} %bitcast.here_ref, s32[1]{0:T(128)} %bitcast.1.group_ref, s32[16]{0:T(128)} %length_ref.3, s32[4]{0:T(128)} %energy_ref.3, s32[4]{0:T(128)} %code_ref.1, f32[24,8,128]{2,1,0:T(8,128)} %shard_map.95.refs_0_, ...), custom_call_target="tpu_custom_call" | custom-call | tf_op jit(solution)/shard_map/pallas_call | solution.py:297
  33.5 1.5 %collective-permute-start.6 = (f32[2,16,512]{2,1,0:T(8,128)}, f32[2,16,512]{2,1,0:T(8,128)S(1)}, u32[]{:S(2)}, u32[]{:S(2)}) collective-permute-start(f32[2,16,512]{2,1,0:T(8,128)} %get-tuple-element.6), channel_id=1, source_target_pairs={{0,1},{1,0},{2,3},{3,2},{4,5},{5,4},{6,7},{7,6},{8,9},{9,8},{10,11... | collective-permute-start | bytes 196616 | tf_op jit(solution)/shard_map/ppermute | solution.py:313
  35.0 3.0 %collective-permute-done.6 = f32[2,16,512]{2,1,0:T(8,128)S(1)} collective-permute-done((f32[2,16,512]{2,1,0:T(8,128)}, f32[2,16,512]{2,1,0:T(8,128)S(1)}, u32[]{:S(2)}, u32[]{:S(2)}) %collective-permute-start.6) | collective-permute-done | bytes 65568 | tf_op jit(solution)/shard_map/ppermute | solution.py:313
  38.0 1.4 %fusion = (f32[16,512]{1,0:T(8,128)}, f32[16,512]{1,0:T(8,128)}) fusion(f32[16,512]{1,0:T(8,128)} %get-tuple-element.7, f32[2,16,512]{2,1,0:T(8,128)S(1)} %collective-permute-done.6, f32[16,512]{1,0:T(8,128)} %get-tuple-element.5), kind=kLoop, calls=%fused_computation.2 | loop fusion | flops 16384 | bytes 196608 | tf_op jit(solution)/shard_map/add | solution.py:314
  (17 shorter events, 0.1 us)
Async XLA Ops:
  0.6 0.8 %copy-start.9 = (f32[4,2,1024]{2,1,0:T(2,128)S(1)}, f32[4,2,1024]{2,1,0:T(2,128)}, u32[]{:S(2)}) copy-start(f32[4,2,1024]{2,1,0:T(2,128)} %param.15) | copy-start | bytes 98308
  0.6 0.9 %copy-start.7 = (f32[16,1024]{1,0:T(8,128)S(1)}, f32[16,1024]{1,0:T(8,128)}, u32[]{:S(2)}) copy-start(f32[16,1024]{1,0:T(8,128)} %param.9) | copy-start | bytes 196612
  1.5 0.7 %copy-start.10 = (f32[1024]{0:T(1024)S(1)}, f32[1024]{0:T(1024)}, u32[]{:S(2)}) copy-start(f32[1024]{0:T(1024)} %param.8) | copy-start | bytes 12292
  2.2 0.8 %copy-start.8 = (f32[16,1024]{1,0:T(8,128)S(1)}, f32[16,1024]{1,0:T(8,128)}, u32[]{:S(2)}) copy-start(f32[16,1024]{1,0:T(8,128)} %param.10) | copy-start | bytes 196612
  3.1 0.7 %copy-start = (f32[48,8,128]{2,1,0:T(8,128)}, f32[48,8,128]{2,1,0:T(8,128)S(1)}, u32[]{:S(2)}) copy-start(f32[48,8,128]{2,1,0:T(8,128)S(1)} %constant_dynamic-update-slice_fusion.table_ref.refs_8_) | copy-start | bytes 589828
  5.7 6.0 %collective-permute-start.2 = (f32[24,8,128]{2,1,0:T(8,128)}, f32[24,8,128]{2,1,0:T(8,128)S(1)}, u32[]{:S(2)}, u32[]{:S(2)}) collective-permute-start(f32[24,8,128]{2,1,0:T(8,128)} %shard_map.95.refs_0_), channel_id=1, source_target_pairs={{0,6},{2,4},{4,2},{6,0},{8,14},{10,12},{12,10},{14,8},{16,22},{18,... | collective-permute-start | bytes 294920 | tf_op jit(solution)/shard_map/ppermute | solution.py:268
  8.3 5.7 %collective-permute-start.1 = (f32[24,8,128]{2,1,0:T(8,128)}, f32[24,8,128]{2,1,0:T(8,128)S(1)}, u32[]{:S(2)}, u32[]{:S(2)}) collective-permute-start(f32[24,8,128]{2,1,0:T(8,128)} %shard_map.95.refs_0_), channel_id=1, source_target_pairs={{0,4},{2,6},{4,0},{6,2},{8,12},{10,14},{12,8},{14,10},{16,20},{18,... | collective-permute-start | bytes 294920 | tf_op jit(solution)/shard_map/ppermute | solution.py:268
  8.5 5.5 %collective-permute-start = (f32[24,8,128]{2,1,0:T(8,128)}, f32[24,8,128]{2,1,0:T(8,128)S(1)}, u32[]{:S(2)}, u32[]{:S(2)}) collective-permute-start(f32[24,8,128]{2,1,0:T(8,128)} %shard_map.95.refs_0_), channel_id=1, source_target_pairs={{0,2},{2,0},{4,6},{6,4},{8,10},{10,8},{12,14},{14,12},{16,18},{18,... | collective-permute-start | bytes 294920 | tf_op jit(solution)/shard_map/ppermute | solution.py:268
  11.7 2.3 %copy-start.1 = (f32[24,8,128]{2,1,0:T(8,128)}, f32[24,8,128]{2,1,0:T(8,128)S(1)}, u32[]{:S(2)}) copy-start(f32[24,8,128]{2,1,0:T(8,128)S(1)} %collective-permute-done.2.refs_3_) | copy-start | bytes 294916
  14.0 0.6 %copy-start.2 = (f32[24,8,128]{2,1,0:T(8,128)}, f32[24,8,128]{2,1,0:T(8,128)S(1)}, u32[]{:S(2)}) copy-start(f32[24,8,128]{2,1,0:T(8,128)S(1)} %collective-permute-done.1.refs_2_) | copy-start | bytes 294916
  14.6 0.6 %copy-start.3 = (f32[24,8,128]{2,1,0:T(8,128)}, f32[24,8,128]{2,1,0:T(8,128)S(1)}, u32[]{:S(2)}) copy-start(f32[24,8,128]{2,1,0:T(8,128)S(1)} %collective-permute-done.refs_1_) | copy-start | bytes 294916
  17.1 7.7 %collective-permute-start.5 = (f32[24,8,128]{2,1,0:T(8,128)}, f32[24,8,128]{2,1,0:T(8,128)S(1)}, u32[]{:S(2)}, u32[]{:S(2)}) collective-permute-start(f32[24,8,128]{2,1,0:T(8,128)} %shard_map.96.refs_4_), channel_id=1, source_target_pairs={{0,24},{2,26},{4,28},{6,30},{8,16},{10,18},{12,20},{14,22},{16,8},... | collective-permute-start | bytes 294920 | tf_op jit(solution)/shard_map/ppermute | solution.py:279
  20.8 9.2 %collective-permute-start.4 = (f32[24,8,128]{2,1,0:T(8,128)}, f32[24,8,128]{2,1,0:T(8,128)S(1)}, u32[]{:S(2)}, u32[]{:S(2)}) collective-permute-start(f32[24,8,128]{2,1,0:T(8,128)} %shard_map.96.refs_4_), channel_id=1, source_target_pairs={{0,16},{2,18},{4,20},{6,22},{8,24},{10,26},{12,28},{14,30},{16,0},... | collective-permute-start | bytes 294920 | tf_op jit(solution)/shard_map/ppermute | solution.py:279
  20.8 9.2 %collective-permute-start.3 = (f32[24,8,128]{2,1,0:T(8,128)}, f32[24,8,128]{2,1,0:T(8,128)S(1)}, u32[]{:S(2)}, u32[]{:S(2)}) collective-permute-start(f32[24,8,128]{2,1,0:T(8,128)} %shard_map.96.refs_4_), channel_id=1, source_target_pairs={{0,8},{2,10},{4,12},{6,14},{8,0},{10,2},{12,4},{14,6},{16,24},{18,... | collective-permute-start | bytes 294920 | tf_op jit(solution)/shard_map/ppermute | solution.py:279
  24.8 5.2 %copy-start.4 = (f32[24,8,128]{2,1,0:T(8,128)}, f32[24,8,128]{2,1,0:T(8,128)S(1)}, u32[]{:S(2)}) copy-start(f32[24,8,128]{2,1,0:T(8,128)S(1)} %collective-permute-done.5.refs_7_) | copy-start | bytes 294916
  30.0 0.6 %copy-start.5 = (f32[24,8,128]{2,1,0:T(8,128)}, f32[24,8,128]{2,1,0:T(8,128)S(1)}, u32[]{:S(2)}) copy-start(f32[24,8,128]{2,1,0:T(8,128)S(1)} %collective-permute-done.4.refs_6_) | copy-start | bytes 294916
  30.0 0.7 %copy-start.6 = (f32[24,8,128]{2,1,0:T(8,128)}, f32[24,8,128]{2,1,0:T(8,128)S(1)}, u32[]{:S(2)}) copy-start(f32[24,8,128]{2,1,0:T(8,128)S(1)} %collective-permute-done.3.refs_5_) | copy-start | bytes 294916
  33.5 4.5 %collective-permute-start.6 = (f32[2,16,512]{2,1,0:T(8,128)}, f32[2,16,512]{2,1,0:T(8,128)S(1)}, u32[]{:S(2)}, u32[]{:S(2)}) collective-permute-start(f32[2,16,512]{2,1,0:T(8,128)} %get-tuple-element.6), channel_id=1, source_target_pairs={{0,1},{1,0},{2,3},{3,2},{4,5},{5,4},{6,7},{7,6},{8,9},{9,8},{10,11... | collective-permute-start | bytes 196616 | tf_op jit(solution)/shard_map/ppermute | solution.py:313

commit v3 on v2

--- a/solution.py
+++ b/solution.py
@@ -69,7 +69,25 @@
     return jnp.stack(onsite_re), jnp.stack(onsite_im)
 
 
-def summary_kernel(here_ref, length_ref, energy_ref, table_ref, out_ref, *, slots, points, devices):
+def build_table(floor_ref, noise_ref, hop_ref, shift_ref, width_ref, table_ref):
+    slots = noise_ref.shape[0]
+    points = shift_ref.shape[0]
+    for row in range(table_ref.shape[1]):
+        lanes = slice(row * 128, (row + 1) * 128)
+        floor = floor_ref[0:1, lanes]
+        for slot in range(slots):
+            table_ref[slot, row:row + 1, :] = floor + noise_ref[slot:slot + 1, lanes]
+            table_ref[slots + slot, row:row + 1, :] = hop_ref[slot:slot + 1, lanes]
+        for point in range(points):
+            for side in range(2):
+                index = 2 * slots + 2 * point + side
+                table_ref[index, row:row + 1, :] = shift_ref[point, side:side + 1, lanes]
+                table_ref[index + 2 * points, row:row + 1, :] = width_ref[point, side:side + 1, lanes]
+
+
+def summary_kernel(here_ref, length_ref, energy_ref, floor_ref, noise_ref, hop_ref, shift_ref, width_ref,
+                   out_ref, table_ref, *, slots, points, devices):
+    build_table(floor_ref, noise_ref, hop_ref, shift_ref, width_ref, table_ref)
     here = here_ref[0]
     count = length_ref[here]
 
@@ -139,7 +157,9 @@
                  slots, points, devices, mixed, size, groups, scale):
     local_refs = refs[:size]
     group_refs = refs[size:size + groups]
-    table_ref, dens_out_ref, bond_out_ref, theirs_ref, left_re_ref, left_im_ref, dens_ref, bond_ref = refs[size + groups:]
+    (floor_ref, noise_ref, hop_ref, shift_ref, width_ref, dens_out_ref, bond_out_ref, theirs_ref,
+     left_re_ref, left_im_ref, dens_ref, bond_ref, table_ref) = refs[size + groups:]
+    build_table(floor_ref, noise_ref, hop_ref, shift_ref, width_ref, table_ref)
     here = here_ref[0]
     count = length_ref[here]
     rows = table_ref.shape[1]
@@ -242,15 +262,8 @@
     here = lax.axis_index("slab")
     devices = lax.axis_size("slab")
     groups = lax.axis_size("energy")
-    table = jnp.concatenate(
-        [
-            mode_floor[None, :] + onsite_noise,
-            hopping,
-            lead_shift.reshape(2 * points, modes),
-            lead_width.reshape(2 * points, modes),
-        ],
-        axis=0,
-    ).reshape(2 * slots + 4 * points, rows, 128)
+    raw = (mode_floor.reshape(1, modes), onsite_noise, hopping, lead_shift, lead_width)
+    table_shape = (2 * slots + 4 * points, rows, 128)
     here_arr = here.astype(jnp.int32).reshape(1)
     smem = pl.BlockSpec(memory_space=pltpu.SMEM)
     vmem = pl.BlockSpec(memory_space=pltpu.VMEM)
@@ -258,9 +271,10 @@
     packed = pl.pallas_call(
         functools.partial(summary_kernel, slots=slots, points=points, devices=devices),
         out_shape=jax.ShapeDtypeStruct((6 * points, rows, 128), jnp.float32),
-        in_specs=[smem, smem, smem, vmem],
+        in_specs=[smem, smem, smem] + [vmem] * len(raw),
         out_specs=vmem,
-    )(here_arr, lengths, energy_index, table)
+        scratch_shapes=[pltpu.VMEM(table_shape, jnp.float32)],
+    )(here_arr, lengths, energy_index, *raw)
     mixed = devices & (devices - 1) == 0 and devices >= 4
     if mixed:
         size = 4
@@ -300,15 +314,16 @@
             size=len(local), groups=len(every), scale=1.0 / (32.0 * points * groups),
         ),
         out_shape=(half, half, jax.ShapeDtypeStruct((2, slots, modes // 2), jnp.float32)),
-        in_specs=[smem] * 5 + [vmem] * (len(local) + len(every) + 1),
+        in_specs=[smem] * 5 + [vmem] * (len(local) + len(every) + len(raw)),
         out_specs=(vmem, vmem, vmem),
         scratch_shapes=[
             pltpu.VMEM((slots, points, rows, 128), jnp.float32),
             pltpu.VMEM((slots, points, rows, 128), jnp.float32),
             pltpu.VMEM((slots, rows, 128), jnp.float32),
             pltpu.VMEM((slots, rows, 128), jnp.float32),
+            pltpu.VMEM(table_shape, jnp.float32),
         ],
-    )(here_arr, group_arr, lengths, energy_index, weight_code, *local, *every, table)
+    )(here_arr, group_arr, lengths, energy_index, weight_code, *local, *every, *raw)
     if groups == 2:
         theirs = lax.ppermute(theirs, "energy", [(0, 1), (1, 0)])
         return (density + theirs[0], bond_density + theirs[1])

time: 39.8 us -> 36.2 us (0.910)
  local copies, waits for them, and re-layouts: 4.93 us -> 1.94 us
  waiting for transfers between devices: 16.9 us -> 15.7 us
  starting transfers between devices: 8.72 us -> 9.69 us
    unnamed x27 -> x12, local copies, waits for them, and re-layouts: 4.08 us -> 1.94 us
    ppermute x3, starting transfers between devices: 2.82 us -> 3.78 us  [shards(): lax.ppermute(packed, 'slab', [(device, device ^ offset) for device in ran...]
    concatenate x3 -> x0, local copies, waits for them, and re-layouts: 0.85 us -> none  [shards(): jnp.concatenate([mode_floor[None, :] + onsite_noise, hopping, lead_shift....]
    ppermute x3, waiting for transfers between devices: 8.53 us -> 7.72 us  [shards(): lax.ppermute(summary, 'slab', [(device, device ^ offset * size) for devic...]
    ppermute x3, waiting for transfers between devices: 5.41 us -> 4.99 us  [shards(): lax.ppermute(packed, 'slab', [(device, device ^ offset) for device in ran...]
where the time goes in v3:
time: 36.2 us; the launch traced here: 35.9 us
  waiting for transfers between devices  15.7 us (43%)
  starting transfers between devices  9.69 us (27%)
  Pallas kernels  6.5 us (18%)
  local copies, waits for them, and re-layouts  1.94 us (5%)
  other arithmetic  1.41 us (4%)
  between operations  0.66 us (2%)
    ppermute x3, waiting for transfers between devices, shards(): lax.ppermute(summary, 'slab', [(device, device ^ offset * size) for devic...  7.72 us
    ppermute x3, waiting for transfers between devices, shards(): lax.ppermute(packed, 'slab', [(device, device ^ offset) for device in ran...  4.99 us
    ppermute x3, starting transfers between devices, shards(): lax.ppermute(summary, 'slab', [(device, device ^ offset * size) for devic...  4.39 us
    ppermute x3, starting transfers between devices, shards(): lax.ppermute(packed, 'slab', [(device, device ^ offset) for device in ran...  3.78 us
    ppermute x1, waiting for transfers between devices, shards(): theirs = lax.ppermute(theirs, 'energy', [(0, 1), (1, 0)])  2.96 us
    pallas_call x1, Pallas kernels, shards(): pl.pallas_call(functools.partial(final_kernel, slots=slots, points=points...  2.77 us
    unnamed x12, local copies, waits for them, and re-layouts  1.94 us
    pallas_call x1, Pallas kernels, shards(): pl.pallas_call(functools.partial(summary_kernel, slots=slots, points=poin...  1.91 us
  transfers between devices with their start and end apart: 7, of which 5 were waited for; matrix products, arithmetic and copies ran while one was open for 0% of the time, Pallas kernels for 0%

profile of v3, /device:TPU:0, one launch (start us, length us, event | category | flops | bytes accessed | tf_op | source)
XLA Modules:
  0.0 35.9 jit_solution(2850763201494452782)
XLA Ops:
  0.6 1.9 %shard_map.95.refs_0_ = f32[24,8,128]{2,1,0:T(8,128)} custom-call(s32[1]{0:T(128)} %bitcast.here_ref, s32[16]{0:T(128)} %length_ref.3, s32[4]{0:T(128)} %energy_ref.3, f32[1,1024]{1,0:T(1,128)} %bitcast.11, f32[16,1024]{1,0:T(8,128)} %refs_9_.1, f32[16,1024]{1,0:T(8,128)} %refs_10_.1, f32[4,2,1024]{2,1,0:T(2,128)} %refs_11_.1, f32[4,2,1024]{2,1,0:T(2,128)} %refs_12_.1), custom_call_target="tpu_custom_call" | custom-call | tf_op jit(solution)/shard_map/pallas_call | solution.py:271
  2.5 3.1 %collective-permute-start.2 = (f32[24,8,128]{2,1,0:T(8,128)}, f32[24,8,128]{2,1,0:T(8,128)S(1)}, u32[]{:S(2)}, u32[]{:S(2)}) collective-permute-start(f32[24,8,128]{2,1,0:T(8,128)} %shard_map.95.refs_0_), channel_id=1, source_target_pairs={{0,6},{2,4},{4,2},{6,0},{8,14},{10,12},{12,10},{14,8},{16,22},{18,... | collective-permute-start | bytes 294920 | tf_op jit(solution)/shard_map/ppermute | solution.py:282
  5.6 0.6 %collective-permute-start.1 = (f32[24,8,128]{2,1,0:T(8,128)}, f32[24,8,128]{2,1,0:T(8,128)S(1)}, u32[]{:S(2)}, u32[]{:S(2)}) collective-permute-start(f32[24,8,128]{2,1,0:T(8,128)} %shard_map.95.refs_0_), channel_id=1, source_target_pairs={{0,4},{2,6},{4,0},{6,2},{8,12},{10,14},{12,8},{14,10},{16,20},{18,... | collective-permute-start | bytes 294920 | tf_op jit(solution)/shard_map/ppermute | solution.py:282
  6.2 0.1 collective-permute-start
  6.3 2.8 %collective-permute-done.2.refs_3_ = f32[24,8,128]{2,1,0:T(8,128)S(1)} collective-permute-done((f32[24,8,128]{2,1,0:T(8,128)}, f32[24,8,128]{2,1,0:T(8,128)S(1)}, u32[]{:S(2)}, u32[]{:S(2)}) %collective-permute-start.2) | collective-permute-done | bytes 98336 | tf_op jit(solution)/shard_map/ppermute | solution.py:282
  9.1 0.0 copy-start
  9.2 2.2 %collective-permute-done.1.refs_2_ = f32[24,8,128]{2,1,0:T(8,128)S(1)} collective-permute-done((f32[24,8,128]{2,1,0:T(8,128)}, f32[24,8,128]{2,1,0:T(8,128)S(1)}, u32[]{:S(2)}, u32[]{:S(2)}) %collective-permute-start.1) | collective-permute-done | bytes 98336 | tf_op jit(solution)/shard_map/ppermute | solution.py:282
  11.3 0.0 copy-start.1
  11.3 0.0 collective-permute-done.refs_1_
  11.3 0.0 copy-done
  11.3 0.6 %copy-done.1 = f32[24,8,128]{2,1,0:T(8,128)} copy-done((f32[24,8,128]{2,1,0:T(8,128)}, f32[24,8,128]{2,1,0:T(8,128)S(1)}, u32[]{:S(2)}) %copy-start.1) | copy-done | bytes 98328
  11.9 0.0 copy-start.2
  11.9 0.6 %copy-done.2 = f32[24,8,128]{2,1,0:T(8,128)} copy-done((f32[24,8,128]{2,1,0:T(8,128)}, f32[24,8,128]{2,1,0:T(8,128)S(1)}, u32[]{:S(2)}) %copy-start.2) | copy-done | bytes 98328
  12.6 1.8 %shard_map.96.refs_4_ = f32[24,8,128]{2,1,0:T(8,128)} custom-call(s32[1]{0:T(128)} %bitcast.here_ref, f32[24,8,128]{2,1,0:T(8,128)} %shard_map.95.refs_0_, f32[24,8,128]{2,1,0:T(8,128)} %copy-done.2, f32[24,8,128]{2,1,0:T(8,128)} %copy-done.1, f32[24,8,128]{2,1,0:T(8,128)} %copy-done), custom_call_target="tpu_custom_call" | custom-call | tf_op jit(solution)/shard_map/pallas_call | solution.py:285
  14.4 3.7 %collective-permute-start.5 = (f32[24,8,128]{2,1,0:T(8,128)}, f32[24,8,128]{2,1,0:T(8,128)S(1)}, u32[]{:S(2)}, u32[]{:S(2)}) collective-permute-start(f32[24,8,128]{2,1,0:T(8,128)} %shard_map.96.refs_4_), channel_id=1, source_target_pairs={{0,24},{2,26},{4,28},{6,30},{8,16},{10,18},{12,20},{14,22},{16,8},... | collective-permute-start | bytes 294920 | tf_op jit(solution)/shard_map/ppermute | solution.py:293
  18.1 0.0 collective-permute-start.4
  18.1 0.7 %collective-permute-start.3 = (f32[24,8,128]{2,1,0:T(8,128)}, f32[24,8,128]{2,1,0:T(8,128)S(1)}, u32[]{:S(2)}, u32[]{:S(2)}) collective-permute-start(f32[24,8,128]{2,1,0:T(8,128)} %shard_map.96.refs_4_), channel_id=1, source_target_pairs={{0,8},{2,10},{4,12},{6,14},{8,0},{10,2},{12,4},{14,6},{16,24},{18,... | collective-permute-start | bytes 294920 | tf_op jit(solution)/shard_map/ppermute | solution.py:293
  18.8 3.4 %collective-permute-done.5.refs_7_ = f32[24,8,128]{2,1,0:T(8,128)S(1)} collective-permute-done((f32[24,8,128]{2,1,0:T(8,128)}, f32[24,8,128]{2,1,0:T(8,128)S(1)}, u32[]{:S(2)}, u32[]{:S(2)}) %collective-permute-start.5) | collective-permute-done | bytes 98336 | tf_op jit(solution)/shard_map/ppermute | solution.py:293
  22.2 0.0 copy-start.3
  22.2 4.3 %collective-permute-done.4.refs_6_ = f32[24,8,128]{2,1,0:T(8,128)S(1)} collective-permute-done((f32[24,8,128]{2,1,0:T(8,128)}, f32[24,8,128]{2,1,0:T(8,128)S(1)}, u32[]{:S(2)}, u32[]{:S(2)}) %collective-permute-start.4) | collective-permute-done | bytes 98336 | tf_op jit(solution)/shard_map/ppermute | solution.py:293
  26.5 0.0 copy-start.4
  26.5 0.0 collective-permute-done.3.refs_5_
  26.5 0.0 copy-start.5
  26.5 0.0 copy-done.3
  26.5 0.6 %copy-done.4 = f32[24,8,128]{2,1,0:T(8,128)} copy-done((f32[24,8,128]{2,1,0:T(8,128)}, f32[24,8,128]{2,1,0:T(8,128)S(1)}, u32[]{:S(2)}) %copy-start.4) | copy-done | bytes 98328
  27.2 0.0 copy-done.5
  27.2 2.8 %shard_map.97 = (f32[16,512]{1,0:T(8,128)}, f32[16,512]{1,0:T(8,128)}, f32[2,16,512]{2,1,0:T(8,128)}) custom-call(s32[1]{0:T(128)} %bitcast.here_ref, s32[1]{0:T(128)} %bitcast.1.group_ref, s32[16]{0:T(128)} %length_ref.3, s32[4]{0:T(128)} %energy_ref.3, s32[4]{0:T(128)} %code_ref.1, f32[24,8,128]{2,1,0:T(8,128)} %shard_map.95.refs_0_, ...), custom_call_target="tpu_custom_call" | custom-call | tf_op jit(solution)/shard_map/pallas_call | solution.py:311
  30.0 1.5 %collective-permute-start.6 = (f32[2,16,512]{2,1,0:T(8,128)}, f32[2,16,512]{2,1,0:T(8,128)S(1)}, u32[]{:S(2)}, u32[]{:S(2)}) collective-permute-start(f32[2,16,512]{2,1,0:T(8,128)} %get-tuple-element.6), channel_id=1, source_target_pairs={{0,1},{1,0},{2,3},{3,2},{4,5},{5,4},{6,7},{7,6},{8,9},{9,8},{10,11... | collective-permute-start | bytes 196616 | tf_op jit(solution)/shard_map/ppermute | solution.py:328
  31.5 3.0 %collective-permute-done.6 = f32[2,16,512]{2,1,0:T(8,128)S(1)} collective-permute-done((f32[2,16,512]{2,1,0:T(8,128)}, f32[2,16,512]{2,1,0:T(8,128)S(1)}, u32[]{:S(2)}, u32[]{:S(2)}) %collective-permute-start.6) | collective-permute-done | bytes 65568 | tf_op jit(solution)/shard_map/ppermute | solution.py:328
  34.4 1.4 %fusion = (f32[16,512]{1,0:T(8,128)}, f32[16,512]{1,0:T(8,128)}) fusion(f32[16,512]{1,0:T(8,128)} %get-tuple-element.7, f32[2,16,512]{2,1,0:T(8,128)S(1)} %collective-permute-done.6, f32[16,512]{1,0:T(8,128)} %get-tuple-element.5), kind=kLoop, calls=%fused_computation.1 | loop fusion | flops 16384 | bytes 196608 | tf_op jit(solution)/shard_map/add | solution.py:329
Async XLA Ops:
  2.5 6.6 %collective-permute-start.2 = (f32[24,8,128]{2,1,0:T(8,128)}, f32[24,8,128]{2,1,0:T(8,128)S(1)}, u32[]{:S(2)}, u32[]{:S(2)}) collective-permute-start(f32[24,8,128]{2,1,0:T(8,128)} %shard_map.95.refs_0_), channel_id=1, source_target_pairs={{0,6},{2,4},{4,2},{6,0},{8,14},{10,12},{12,10},{14,8},{16,22},{18,... | collective-permute-start | bytes 294920 | tf_op jit(solution)/shard_map/ppermute | solution.py:282
  5.6 5.7 %collective-permute-start.1 = (f32[24,8,128]{2,1,0:T(8,128)}, f32[24,8,128]{2,1,0:T(8,128)S(1)}, u32[]{:S(2)}, u32[]{:S(2)}) collective-permute-start(f32[24,8,128]{2,1,0:T(8,128)} %shard_map.95.refs_0_), channel_id=1, source_target_pairs={{0,4},{2,6},{4,0},{6,2},{8,12},{10,14},{12,8},{14,10},{16,20},{18,... | collective-permute-start | bytes 294920 | tf_op jit(solution)/shard_map/ppermute | solution.py:282
  6.2 5.1 %collective-permute-start = (f32[24,8,128]{2,1,0:T(8,128)}, f32[24,8,128]{2,1,0:T(8,128)S(1)}, u32[]{:S(2)}, u32[]{:S(2)}) collective-permute-start(f32[24,8,128]{2,1,0:T(8,128)} %shard_map.95.refs_0_), channel_id=1, source_target_pairs={{0,2},{2,0},{4,6},{6,4},{8,10},{10,8},{12,14},{14,12},{16,18},{18,... | collective-permute-start | bytes 294920 | tf_op jit(solution)/shard_map/ppermute | solution.py:282
  9.1 2.2 %copy-start = (f32[24,8,128]{2,1,0:T(8,128)}, f32[24,8,128]{2,1,0:T(8,128)S(1)}, u32[]{:S(2)}) copy-start(f32[24,8,128]{2,1,0:T(8,128)S(1)} %collective-permute-done.2.refs_3_) | copy-start | bytes 294916
  11.3 0.6 %copy-start.1 = (f32[24,8,128]{2,1,0:T(8,128)}, f32[24,8,128]{2,1,0:T(8,128)S(1)}, u32[]{:S(2)}) copy-start(f32[24,8,128]{2,1,0:T(8,128)S(1)} %collective-permute-done.1.refs_2_) | copy-start | bytes 294916
  11.9 0.6 %copy-start.2 = (f32[24,8,128]{2,1,0:T(8,128)}, f32[24,8,128]{2,1,0:T(8,128)S(1)}, u32[]{:S(2)}) copy-start(f32[24,8,128]{2,1,0:T(8,128)S(1)} %collective-permute-done.refs_1_) | copy-start | bytes 294916
  14.4 7.8 %collective-permute-start.5 = (f32[24,8,128]{2,1,0:T(8,128)}, f32[24,8,128]{2,1,0:T(8,128)S(1)}, u32[]{:S(2)}, u32[]{:S(2)}) collective-permute-start(f32[24,8,128]{2,1,0:T(8,128)} %shard_map.96.refs_4_), channel_id=1, source_target_pairs={{0,24},{2,26},{4,28},{6,30},{8,16},{10,18},{12,20},{14,22},{16,8},... | collective-permute-start | bytes 294920 | tf_op jit(solution)/shard_map/ppermute | solution.py:293
  18.1 8.4 %collective-permute-start.4 = (f32[24,8,128]{2,1,0:T(8,128)}, f32[24,8,128]{2,1,0:T(8,128)S(1)}, u32[]{:S(2)}, u32[]{:S(2)}) collective-permute-start(f32[24,8,128]{2,1,0:T(8,128)} %shard_map.96.refs_4_), channel_id=1, source_target_pairs={{0,16},{2,18},{4,20},{6,22},{8,24},{10,26},{12,28},{14,30},{16,0},... | collective-permute-start | bytes 294920 | tf_op jit(solution)/shard_map/ppermute | solution.py:293
  18.1 8.4 %collective-permute-start.3 = (f32[24,8,128]{2,1,0:T(8,128)}, f32[24,8,128]{2,1,0:T(8,128)S(1)}, u32[]{:S(2)}, u32[]{:S(2)}) collective-permute-start(f32[24,8,128]{2,1,0:T(8,128)} %shard_map.96.refs_4_), channel_id=1, source_target_pairs={{0,8},{2,10},{4,12},{6,14},{8,0},{10,2},{12,4},{14,6},{16,24},{18,... | collective-permute-start | bytes 294920 | tf_op jit(solution)/shard_map/ppermute | solution.py:293
  22.2 4.4 %copy-start.3 = (f32[24,8,128]{2,1,0:T(8,128)}, f32[24,8,128]{2,1,0:T(8,128)S(1)}, u32[]{:S(2)}) copy-start(f32[24,8,128]{2,1,0:T(8,128)S(1)} %collective-permute-done.5.refs_7_) | copy-start | bytes 294916
  26.5 0.6 %copy-start.4 = (f32[24,8,128]{2,1,0:T(8,128)}, f32[24,8,128]{2,1,0:T(8,128)S(1)}, u32[]{:S(2)}) copy-start(f32[24,8,128]{2,1,0:T(8,128)S(1)} %collective-permute-done.4.refs_6_) | copy-start | bytes 294916
  26.5 0.7 %copy-start.5 = (f32[24,8,128]{2,1,0:T(8,128)}, f32[24,8,128]{2,1,0:T(8,128)S(1)}, u32[]{:S(2)}) copy-start(f32[24,8,128]{2,1,0:T(8,128)S(1)} %collective-permute-done.3.refs_5_) | copy-start | bytes 294916
  30.0 4.5 %collective-permute-start.6 = (f32[2,16,512]{2,1,0:T(8,128)}, f32[2,16,512]{2,1,0:T(8,128)S(1)}, u32[]{:S(2)}, u32[]{:S(2)}) collective-permute-start(f32[2,16,512]{2,1,0:T(8,128)} %get-tuple-element.6), channel_id=1, source_target_pairs={{0,1},{1,0},{2,3},{3,2},{4,5},{5,4},{6,7},{7,6},{8,9},{9,8},{10,11... | collective-permute-start | bytes 196616 | tf_op jit(solution)/shard_map/ppermute | solution.py:328

commit v4 on v3

--- a/solution.py
+++ b/solution.py
@@ -157,9 +157,8 @@
                  slots, points, devices, mixed, size, groups, scale):
     local_refs = refs[:size]
     group_refs = refs[size:size + groups]
-    (floor_ref, noise_ref, hop_ref, shift_ref, width_ref, dens_out_ref, bond_out_ref, theirs_ref,
-     left_re_ref, left_im_ref, dens_ref, bond_ref, table_ref) = refs[size + groups:]
-    build_table(floor_ref, noise_ref, hop_ref, shift_ref, width_ref, table_ref)
+    (table_ref, dens_out_ref, bond_out_ref, theirs_ref,
+     left_re_ref, left_im_ref, dens_ref, bond_ref) = refs[size + groups:]
     here = here_ref[0]
     count = length_ref[here]
     rows = table_ref.shape[1]
@@ -268,12 +267,14 @@
     smem = pl.BlockSpec(memory_space=pltpu.SMEM)
     vmem = pl.BlockSpec(memory_space=pltpu.VMEM)
 
-    packed = pl.pallas_call(
+    packed, table = pl.pallas_call(
         functools.partial(summary_kernel, slots=slots, points=points, devices=devices),
-        out_shape=jax.ShapeDtypeStruct((6 * points, rows, 128), jnp.float32),
+        out_shape=(
+            jax.ShapeDtypeStruct((6 * points, rows, 128), jnp.float32),
+            jax.ShapeDtypeStruct(table_shape, jnp.float32),
+        ),
         in_specs=[smem, smem, smem] + [vmem] * len(raw),
-        out_specs=vmem,
-        scratch_shapes=[pltpu.VMEM(table_shape, jnp.float32)],
+        out_specs=(vmem, vmem),
     )(here_arr, lengths, energy_index, *raw)
     mixed = devices & (devices - 1) == 0 and devices >= 4
     if mixed:
@@ -314,16 +315,15 @@
             size=len(local), groups=len(every), scale=1.0 / (32.0 * points * groups),
         ),
         out_shape=(half, half, jax.ShapeDtypeStruct((2, slots, modes // 2), jnp.float32)),
-        in_specs=[smem] * 5 + [vmem] * (len(local) + len(every) + len(raw)),
+        in_specs=[smem] * 5 + [vmem] * (len(local) + len(every) + 1),
         out_specs=(vmem, vmem, vmem),
         scratch_shapes=[
             pltpu.VMEM((slots, points, rows, 128), jnp.float32),
             pltpu.VMEM((slots, points, rows, 128), jnp.float32),
             pltpu.VMEM((slots, rows, 128), jnp.float32),
             pltpu.VMEM((slots, rows, 128), jnp.float32),
-            pltpu.VMEM(table_shape, jnp.float32),
         ],
-    )(here_arr, group_arr, lengths, energy_index, weight_code, *local, *every, *raw)
+    )(here_arr, group_arr, lengths, energy_index, weight_code, *local, *every, table)
     if groups == 2:
         theirs = lax.ppermute(theirs, "energy", [(0, 1), (1, 0)])
         return (density + theirs[0], bond_density + theirs[1])

time: 36.2 us -> 36.6 us (1.011)
  waiting for transfers between devices: 15.7 us -> 16.1 us
    ppermute x3, waiting for transfers between devices: 7.72 us -> 8.42 us  [shards(): lax.ppermute(summary, 'slab', [(device, device ^ offset * size) for devic...]
where the time goes in v4:
time: 36.6 us; the launch traced here: 36.2 us
  waiting for transfers between devices  16.1 us (44%)
  starting transfers between devices  9.93 us (27%)
  Pallas kernels  6.21 us (17%)
  local copies, waits for them, and re-layouts  1.94 us (5%)
  other arithmetic  1.41 us (4%)
  between operations  0.66 us (2%)
    ppermute x3, waiting for transfers between devices, shards(): lax.ppermute(summary, 'slab', [(device, device ^ offset * size) for devic...  8.42 us
    ppermute x3, waiting for transfers between devices, shards(): lax.ppermute(packed, 'slab', [(device, device ^ offset) for device in ran...  4.65 us
    ppermute x3, starting transfers between devices, shards(): lax.ppermute(summary, 'slab', [(device, device ^ offset * size) for devic...  4.51 us
    ppermute x3, starting transfers between devices, shards(): lax.ppermute(packed, 'slab', [(device, device ^ offset) for device in ran...  3.91 us
    ppermute x1, waiting for transfers between devices, shards(): theirs = lax.ppermute(theirs, 'energy', [(0, 1), (1, 0)])  3.02 us
    pallas_call x1, Pallas kernels, shards(): pl.pallas_call(functools.partial(final_kernel, slots=slots, points=points...  2.54 us
    unnamed x12, local copies, waits for them, and re-layouts  1.94 us
    pallas_call x1, Pallas kernels, shards(): pl.pallas_call(functools.partial(summary_kernel, slots=slots, points=poin...  1.85 us
  transfers between devices with their start and end apart: 7, of which 5 were waited for; matrix products, arithmetic and copies ran while one was open for 0% of the time, Pallas kernels for 0%

profile of v4, /device:TPU:0, one launch (start us, length us, event | category | flops | bytes accessed | tf_op | source)
XLA Modules:
  0.0 36.2 jit_solution(13090888811893864464)
XLA Ops:
  0.6 1.9 %shard_map.95 = (f32[24,8,128]{2,1,0:T(8,128)}, f32[48,8,128]{2,1,0:T(8,128)}) custom-call(s32[1]{0:T(128)} %bitcast.here_ref, s32[16]{0:T(128)} %length_ref.3, s32[4]{0:T(128)} %energy_ref.3, f32[1,1024]{1,0:T(1,128)} %bitcast.11, f32[16,1024]{1,0:T(8,128)} %noise_ref.1, f32[16,1024]{1,0:T(8,128)} %hop_ref.1, f32[4,2,1024]{2,1,0:T(2,128)} %shift_ref.1, ...), custom_call_target="tpu_custom_call" | custom-call | tf_op jit(solution)/shard_map/pallas_call | solution.py:270
  2.5 2.8 %collective-permute-start.2 = (f32[24,8,128]{2,1,0:T(8,128)}, f32[24,8,128]{2,1,0:T(8,128)S(1)}, u32[]{:S(2)}, u32[]{:S(2)}) collective-permute-start(f32[24,8,128]{2,1,0:T(8,128)} %get-tuple-element.7.refs_0_), channel_id=1, source_target_pairs={{0,6},{2,4},{4,2},{6,0},{8,14},{10,12},{12,10},{14,8},{16,22},{18,... | collective-permute-start | bytes 294920 | tf_op jit(solution)/shard_map/ppermute | solution.py:283
  5.3 1.0 %collective-permute-start.1 = (f32[24,8,128]{2,1,0:T(8,128)}, f32[24,8,128]{2,1,0:T(8,128)S(1)}, u32[]{:S(2)}, u32[]{:S(2)}) collective-permute-start(f32[24,8,128]{2,1,0:T(8,128)} %get-tuple-element.7.refs_0_), channel_id=1, source_target_pairs={{0,4},{2,6},{4,0},{6,2},{8,12},{10,14},{12,8},{14,10},{16,20},{18,... | collective-permute-start | bytes 294920 | tf_op jit(solution)/shard_map/ppermute | solution.py:283
  6.3 0.1 collective-permute-start
  6.4 2.1 %collective-permute-done.2.refs_3_ = f32[24,8,128]{2,1,0:T(8,128)S(1)} collective-permute-done((f32[24,8,128]{2,1,0:T(8,128)}, f32[24,8,128]{2,1,0:T(8,128)S(1)}, u32[]{:S(2)}, u32[]{:S(2)}) %collective-permute-start.2) | collective-permute-done | bytes 98336 | tf_op jit(solution)/shard_map/ppermute | solution.py:283
  8.5 0.0 copy-start
  8.5 2.6 %collective-permute-done.1.refs_2_ = f32[24,8,128]{2,1,0:T(8,128)S(1)} collective-permute-done((f32[24,8,128]{2,1,0:T(8,128)}, f32[24,8,128]{2,1,0:T(8,128)S(1)}, u32[]{:S(2)}, u32[]{:S(2)}) %collective-permute-start.1) | collective-permute-done | bytes 98336 | tf_op jit(solution)/shard_map/ppermute | solution.py:283
  11.1 0.0 copy-start.1
  11.1 0.0 collective-permute-done.refs_1_
  11.1 0.0 copy-done
  11.1 0.6 %copy-done.1 = f32[24,8,128]{2,1,0:T(8,128)} copy-done((f32[24,8,128]{2,1,0:T(8,128)}, f32[24,8,128]{2,1,0:T(8,128)S(1)}, u32[]{:S(2)}) %copy-start.1) | copy-done | bytes 98328
  11.7 0.0 copy-start.2
  11.7 0.6 %copy-done.2 = f32[24,8,128]{2,1,0:T(8,128)} copy-done((f32[24,8,128]{2,1,0:T(8,128)}, f32[24,8,128]{2,1,0:T(8,128)S(1)}, u32[]{:S(2)}) %copy-start.2) | copy-done | bytes 98328
  12.3 1.8 %shard_map.96.refs_4_ = f32[24,8,128]{2,1,0:T(8,128)} custom-call(s32[1]{0:T(128)} %bitcast.here_ref, f32[24,8,128]{2,1,0:T(8,128)} %get-tuple-element.7.refs_0_, f32[24,8,128]{2,1,0:T(8,128)} %copy-done.2, f32[24,8,128]{2,1,0:T(8,128)} %copy-done.1, f32[24,8,128]{2,1,0:T(8,128)} %copy-done), custom_call_target="tpu_custom_call" | custom-call | tf_op jit(solution)/shard_map/pallas_call | solution.py:286
  14.1 3.9 %collective-permute-start.5 = (f32[24,8,128]{2,1,0:T(8,128)}, f32[24,8,128]{2,1,0:T(8,128)S(1)}, u32[]{:S(2)}, u32[]{:S(2)}) collective-permute-start(f32[24,8,128]{2,1,0:T(8,128)} %shard_map.96.refs_4_), channel_id=1, source_target_pairs={{0,24},{2,26},{4,28},{6,30},{8,16},{10,18},{12,20},{14,22},{16,8},... | collective-permute-start | bytes 294920 | tf_op jit(solution)/shard_map/ppermute | solution.py:294
  18.1 0.0 collective-permute-start.4
  18.1 0.6 %collective-permute-start.3 = (f32[24,8,128]{2,1,0:T(8,128)}, f32[24,8,128]{2,1,0:T(8,128)S(1)}, u32[]{:S(2)}, u32[]{:S(2)}) collective-permute-start(f32[24,8,128]{2,1,0:T(8,128)} %shard_map.96.refs_4_), channel_id=1, source_target_pairs={{0,8},{2,10},{4,12},{6,14},{8,0},{10,2},{12,4},{14,6},{16,24},{18,... | collective-permute-start | bytes 294920 | tf_op jit(solution)/shard_map/ppermute | solution.py:294
  18.7 2.9 %collective-permute-done.5.refs_7_ = f32[24,8,128]{2,1,0:T(8,128)S(1)} collective-permute-done((f32[24,8,128]{2,1,0:T(8,128)}, f32[24,8,128]{2,1,0:T(8,128)S(1)}, u32[]{:S(2)}, u32[]{:S(2)}) %collective-permute-start.5) | collective-permute-done | bytes 98336 | tf_op jit(solution)/shard_map/ppermute | solution.py:294
  21.6 0.0 copy-start.3
  21.6 5.5 %collective-permute-done.4.refs_6_ = f32[24,8,128]{2,1,0:T(8,128)S(1)} collective-permute-done((f32[24,8,128]{2,1,0:T(8,128)}, f32[24,8,128]{2,1,0:T(8,128)S(1)}, u32[]{:S(2)}, u32[]{:S(2)}) %collective-permute-start.4) | collective-permute-done | bytes 98336 | tf_op jit(solution)/shard_map/ppermute | solution.py:294
  27.1 0.0 copy-start.4
  27.1 0.0 collective-permute-done.3.refs_5_
  27.1 0.0 copy-start.5
  27.1 0.0 copy-done.3
  27.1 0.6 %copy-done.4 = f32[24,8,128]{2,1,0:T(8,128)} copy-done((f32[24,8,128]{2,1,0:T(8,128)}, f32[24,8,128]{2,1,0:T(8,128)S(1)}, u32[]{:S(2)}) %copy-start.4) | copy-done | bytes 98328
  27.7 0.0 copy-done.5
  27.8 2.5 %shard_map.97 = (f32[16,512]{1,0:T(8,128)}, f32[16,512]{1,0:T(8,128)}, f32[2,16,512]{2,1,0:T(8,128)}) custom-call(s32[1]{0:T(128)} %bitcast.here_ref, s32[1]{0:T(128)} %bitcast.1.group_ref, s32[16]{0:T(128)} %length_ref.3, s32[4]{0:T(128)} %energy_ref.3, s32[4]{0:T(128)} %code_ref.1, f32[24,8,128]{2,1,0:T(8,128)} %get-tuple-element.7.refs_0_, ...), custom_call_target="tpu_custom_call" | custom-call | tf_op jit(solution)/shard_map/pallas_call | solution.py:312
  30.3 1.5 %collective-permute-start.6 = (f32[2,16,512]{2,1,0:T(8,128)}, f32[2,16,512]{2,1,0:T(8,128)S(1)}, u32[]{:S(2)}, u32[]{:S(2)}) collective-permute-start(f32[2,16,512]{2,1,0:T(8,128)} %get-tuple-element.10), channel_id=1, source_target_pairs={{0,1},{1,0},{2,3},{3,2},{4,5},{5,4},{6,7},{7,6},{8,9},{9,8},{10,11... | collective-permute-start | bytes 196616 | tf_op jit(solution)/shard_map/ppermute | solution.py:328
  31.8 3.0 %collective-permute-done.6 = f32[2,16,512]{2,1,0:T(8,128)S(1)} collective-permute-done((f32[2,16,512]{2,1,0:T(8,128)}, f32[2,16,512]{2,1,0:T(8,128)S(1)}, u32[]{:S(2)}, u32[]{:S(2)}) %collective-permute-start.6) | collective-permute-done | bytes 65568 | tf_op jit(solution)/shard_map/ppermute | solution.py:328
  34.8 1.4 %fusion = (f32[16,512]{1,0:T(8,128)}, f32[16,512]{1,0:T(8,128)}) fusion(f32[16,512]{1,0:T(8,128)} %get-tuple-element.11, f32[2,16,512]{2,1,0:T(8,128)S(1)} %collective-permute-done.6, f32[16,512]{1,0:T(8,128)} %get-tuple-element.9), kind=kLoop, calls=%fused_computation.1 | loop fusion | flops 16384 | bytes 196608 | tf_op jit(solution)/shard_map/add | solution.py:329
Async XLA Ops:
  2.5 6.0 %collective-permute-start.2 = (f32[24,8,128]{2,1,0:T(8,128)}, f32[24,8,128]{2,1,0:T(8,128)S(1)}, u32[]{:S(2)}, u32[]{:S(2)}) collective-permute-start(f32[24,8,128]{2,1,0:T(8,128)} %get-tuple-element.7.refs_0_), channel_id=1, source_target_pairs={{0,6},{2,4},{4,2},{6,0},{8,14},{10,12},{12,10},{14,8},{16,22},{18,... | collective-permute-start | bytes 294920 | tf_op jit(solution)/shard_map/ppermute | solution.py:283
  5.3 5.8 %collective-permute-start.1 = (f32[24,8,128]{2,1,0:T(8,128)}, f32[24,8,128]{2,1,0:T(8,128)S(1)}, u32[]{:S(2)}, u32[]{:S(2)}) collective-permute-start(f32[24,8,128]{2,1,0:T(8,128)} %get-tuple-element.7.refs_0_), channel_id=1, source_target_pairs={{0,4},{2,6},{4,0},{6,2},{8,12},{10,14},{12,8},{14,10},{16,20},{18,... | collective-permute-start | bytes 294920 | tf_op jit(solution)/shard_map/ppermute | solution.py:283
  6.3 4.7 %collective-permute-start = (f32[24,8,128]{2,1,0:T(8,128)}, f32[24,8,128]{2,1,0:T(8,128)S(1)}, u32[]{:S(2)}, u32[]{:S(2)}) collective-permute-start(f32[24,8,128]{2,1,0:T(8,128)} %get-tuple-element.7.refs_0_), channel_id=1, source_target_pairs={{0,2},{2,0},{4,6},{6,4},{8,10},{10,8},{12,14},{14,12},{16,18},{18,... | collective-permute-start | bytes 294920 | tf_op jit(solution)/shard_map/ppermute | solution.py:283
  8.5 2.6 %copy-start = (f32[24,8,128]{2,1,0:T(8,128)}, f32[24,8,128]{2,1,0:T(8,128)S(1)}, u32[]{:S(2)}) copy-start(f32[24,8,128]{2,1,0:T(8,128)S(1)} %collective-permute-done.2.refs_3_) | copy-start | bytes 294916
  11.1 0.6 %copy-start.1 = (f32[24,8,128]{2,1,0:T(8,128)}, f32[24,8,128]{2,1,0:T(8,128)S(1)}, u32[]{:S(2)}) copy-start(f32[24,8,128]{2,1,0:T(8,128)S(1)} %collective-permute-done.1.refs_2_) | copy-start | bytes 294916
  11.7 0.6 %copy-start.2 = (f32[24,8,128]{2,1,0:T(8,128)}, f32[24,8,128]{2,1,0:T(8,128)S(1)}, u32[]{:S(2)}) copy-start(f32[24,8,128]{2,1,0:T(8,128)S(1)} %collective-permute-done.refs_1_) | copy-start | bytes 294916
  14.1 7.5 %collective-permute-start.5 = (f32[24,8,128]{2,1,0:T(8,128)}, f32[24,8,128]{2,1,0:T(8,128)S(1)}, u32[]{:S(2)}, u32[]{:S(2)}) collective-permute-start(f32[24,8,128]{2,1,0:T(8,128)} %shard_map.96.refs_4_), channel_id=1, source_target_pairs={{0,24},{2,26},{4,28},{6,30},{8,16},{10,18},{12,20},{14,22},{16,8},... | collective-permute-start | bytes 294920 | tf_op jit(solution)/shard_map/ppermute | solution.py:294
  18.1 9.0 %collective-permute-start.4 = (f32[24,8,128]{2,1,0:T(8,128)}, f32[24,8,128]{2,1,0:T(8,128)S(1)}, u32[]{:S(2)}, u32[]{:S(2)}) collective-permute-start(f32[24,8,128]{2,1,0:T(8,128)} %shard_map.96.refs_4_), channel_id=1, source_target_pairs={{0,16},{2,18},{4,20},{6,22},{8,24},{10,26},{12,28},{14,30},{16,0},... | collective-permute-start | bytes 294920 | tf_op jit(solution)/shard_map/ppermute | solution.py:294
  18.1 9.0 %collective-permute-start.3 = (f32[24,8,128]{2,1,0:T(8,128)}, f32[24,8,128]{2,1,0:T(8,128)S(1)}, u32[]{:S(2)}, u32[]{:S(2)}) collective-permute-start(f32[24,8,128]{2,1,0:T(8,128)} %shard_map.96.refs_4_), channel_id=1, source_target_pairs={{0,8},{2,10},{4,12},{6,14},{8,0},{10,2},{12,4},{14,6},{16,24},{18,... | collective-permute-start | bytes 294920 | tf_op jit(solution)/shard_map/ppermute | solution.py:294
  21.6 5.5 %copy-start.3 = (f32[24,8,128]{2,1,0:T(8,128)}, f32[24,8,128]{2,1,0:T(8,128)S(1)}, u32[]{:S(2)}) copy-start(f32[24,8,128]{2,1,0:T(8,128)S(1)} %collective-permute-done.5.refs_7_) | copy-start | bytes 294916
  27.1 0.6 %copy-start.4 = (f32[24,8,128]{2,1,0:T(8,128)}, f32[24,8,128]{2,1,0:T(8,128)S(1)}, u32[]{:S(2)}) copy-start(f32[24,8,128]{2,1,0:T(8,128)S(1)} %collective-permute-done.4.refs_6_) | copy-start | bytes 294916
  27.1 0.7 %copy-start.5 = (f32[24,8,128]{2,1,0:T(8,128)}, f32[24,8,128]{2,1,0:T(8,128)S(1)}, u32[]{:S(2)}) copy-start(f32[24,8,128]{2,1,0:T(8,128)S(1)} %collective-permute-done.3.refs_5_) | copy-start | bytes 294916
  30.3 4.5 %collective-permute-start.6 = (f32[2,16,512]{2,1,0:T(8,128)}, f32[2,16,512]{2,1,0:T(8,128)S(1)}, u32[]{:S(2)}, u32[]{:S(2)}) collective-permute-start(f32[2,16,512]{2,1,0:T(8,128)} %get-tuple-element.10), channel_id=1, source_target_pairs={{0,1},{1,0},{2,3},{3,2},{4,5},{5,4},{6,7},{7,6},{8,9},{9,8},{10,11... | collective-permute-start | bytes 196616 | tf_op jit(solution)/shard_map/ppermute | solution.py:328

commit v5 on v3

--- a/solution.py
+++ b/solution.py
@@ -144,13 +144,17 @@
     local_refs, out_ref = refs[:-1], refs[-1]
     points = out_ref.shape[0] // 6
     size = len(local_refs)
-    here = here_ref[0]
-    blocks = in_order(local_refs, jnp.bitwise_and(here, size - 1), True)
-    summary = split_fields(blocks[0], points)
-    for member in range(1, size):
-        summary = join_coupled(summary, split_fields(blocks[member], points))
-    for index, value in enumerate(summary):
-        out_ref[index * points:(index + 1) * points] = value
+    own = jnp.bitwise_and(here_ref[0], size - 1)
+    for offset in range(size):
+
+        @pl.when(own == offset)
+        def _(offset=offset):
+            summary = split_fields(local_refs[offset][...], points)
+            for member in range(1, size):
+                block = split_fields(local_refs[member ^ offset][...], points)
+                summary = join_coupled(summary, block)
+            for index, value in enumerate(summary):
+                out_ref[index * points:(index + 1) * points] = value
 
 
 def final_kernel(here_ref, group_ref, length_ref, energy_ref, code_ref, *refs,

time: 36.2 us -> 36.4 us (level)
  waiting for transfers between devices: 15.7 us -> 16.7 us
  Pallas kernels: 6.5 us -> 6.1 us
    ppermute x3, waiting for transfers between devices: 4.99 us -> 5.52 us  [shards(): lax.ppermute(packed, 'slab', [(device, device ^ offset) for device in ran...]
    ppermute x3, waiting for transfers between devices: 7.72 us -> 8.24 us  [shards(): lax.ppermute(summary, 'slab', [(device, device ^ offset * size) for devic...]
where the time goes in v5:
time: 36.4 us; the launch traced here: 36.2 us
  waiting for transfers between devices  16.7 us (46%)
  starting transfers between devices  9.34 us (26%)
  Pallas kernels  6.1 us (17%)
  local copies, waits for them, and re-layouts  1.94 us (5%)
  other arithmetic  1.41 us (4%)
  between operations  0.66 us (2%)
    ppermute x3, waiting for transfers between devices, shards(): lax.ppermute(summary, 'slab', [(device, device ^ offset * size) for devic...  8.24 us
    ppermute x3, waiting for transfers between devices, shards(): lax.ppermute(packed, 'slab', [(device, device ^ offset) for device in ran...  5.52 us
    ppermute x3, starting transfers between devices, shards(): lax.ppermute(summary, 'slab', [(device, device ^ offset * size) for devic...  4.39 us
    ppermute x3, starting transfers between devices, shards(): lax.ppermute(packed, 'slab', [(device, device ^ offset) for device in ran...  3.43 us
    ppermute x1, waiting for transfers between devices, shards(): theirs = lax.ppermute(theirs, 'energy', [(0, 1), (1, 0)])  2.96 us
    pallas_call x1, Pallas kernels, shards(): pl.pallas_call(functools.partial(final_kernel, slots=slots, points=points...  2.59 us
    unnamed x12, local copies, waits for them, and re-layouts  1.94 us
    pallas_call x1, Pallas kernels, shards(): pl.pallas_call(group_kernel, out_shape=jax.ShapeDtypeStruct(packed.shape,...  1.78 us
  transfers between devices with their start and end apart: 7, of which 5 were waited for; matrix products, arithmetic and copies ran while one was open for 0% of the time, Pallas kernels for 0%

profile of v5, /device:TPU:0, one launch (start us, length us, event | category | flops | bytes accessed | tf_op | source)
XLA Modules:
  0.0 36.2 jit_solution(14207104243831495994)
XLA Ops:
  0.6 1.7 %shard_map.95.refs_0_ = f32[24,8,128]{2,1,0:T(8,128)} custom-call(s32[1]{0:T(128)} %bitcast.here_ref, s32[16]{0:T(128)} %length_ref.3, s32[4]{0:T(128)} %energy_ref.3, f32[1,1024]{1,0:T(1,128)} %bitcast.11, f32[16,1024]{1,0:T(8,128)} %refs_9_.1, f32[16,1024]{1,0:T(8,128)} %refs_10_.1, f32[4,2,1024]{2,1,0:T(2,128)} %refs_11_.1, f32[4,2,1024]{2,1,0:T(2,128)} %refs_12_.1), custom_call_target="tpu_custom_call" | custom-call | tf_op jit(solution)/shard_map/pallas_call | solution.py:275
  2.4 3.3 %collective-permute-start.2 = (f32[24,8,128]{2,1,0:T(8,128)}, f32[24,8,128]{2,1,0:T(8,128)S(1)}, u32[]{:S(2)}, u32[]{:S(2)}) collective-permute-start(f32[24,8,128]{2,1,0:T(8,128)} %shard_map.95.refs_0_), channel_id=1, source_target_pairs={{0,6},{2,4},{4,2},{6,0},{8,14},{10,12},{12,10},{14,8},{16,22},{18,... | collective-permute-start | bytes 294920 | tf_op jit(solution)/shard_map/ppermute | solution.py:286
  5.6 0.0 collective-permute-start.1
  5.7 0.1 collective-permute-start
  5.8 3.3 %collective-permute-done.2.refs_3_ = f32[24,8,128]{2,1,0:T(8,128)S(1)} collective-permute-done((f32[24,8,128]{2,1,0:T(8,128)}, f32[24,8,128]{2,1,0:T(8,128)S(1)}, u32[]{:S(2)}, u32[]{:S(2)}) %collective-permute-start.2) | collective-permute-done | bytes 98336 | tf_op jit(solution)/shard_map/ppermute | solution.py:286
  9.1 0.0 copy-start
  9.1 2.2 %collective-permute-done.1.refs_2_ = f32[24,8,128]{2,1,0:T(8,128)S(1)} collective-permute-done((f32[24,8,128]{2,1,0:T(8,128)}, f32[24,8,128]{2,1,0:T(8,128)S(1)}, u32[]{:S(2)}, u32[]{:S(2)}) %collective-permute-start.1) | collective-permute-done | bytes 98336 | tf_op jit(solution)/shard_map/ppermute | solution.py:286
  11.3 0.0 copy-start.1
  11.3 0.0 collective-permute-done.refs_1_
  11.3 0.0 copy-done
  11.3 0.6 %copy-done.1 = f32[24,8,128]{2,1,0:T(8,128)} copy-done((f32[24,8,128]{2,1,0:T(8,128)}, f32[24,8,128]{2,1,0:T(8,128)S(1)}, u32[]{:S(2)}) %copy-start.1) | copy-done | bytes 98328
  11.9 0.0 copy-start.2
  11.9 0.6 %copy-done.2 = f32[24,8,128]{2,1,0:T(8,128)} copy-done((f32[24,8,128]{2,1,0:T(8,128)}, f32[24,8,128]{2,1,0:T(8,128)S(1)}, u32[]{:S(2)}) %copy-start.2) | copy-done | bytes 98328
  12.6 1.8 %shard_map.96.refs_4_ = f32[24,8,128]{2,1,0:T(8,128)} custom-call(s32[1]{0:T(128)} %bitcast.here_ref, f32[24,8,128]{2,1,0:T(8,128)} %shard_map.95.refs_0_, f32[24,8,128]{2,1,0:T(8,128)} %copy-done.2, f32[24,8,128]{2,1,0:T(8,128)} %copy-done.1, f32[24,8,128]{2,1,0:T(8,128)} %copy-done), custom_call_target="tpu_custom_call" | custom-call | tf_op jit(solution)/shard_map/pallas_call | solution.py:289
  14.4 3.5 %collective-permute-start.5 = (f32[24,8,128]{2,1,0:T(8,128)}, f32[24,8,128]{2,1,0:T(8,128)S(1)}, u32[]{:S(2)}, u32[]{:S(2)}) collective-permute-start(f32[24,8,128]{2,1,0:T(8,128)} %shard_map.96.refs_4_), channel_id=1, source_target_pairs={{0,24},{2,26},{4,28},{6,30},{8,16},{10,18},{12,20},{14,22},{16,8},... | collective-permute-start | bytes 294920 | tf_op jit(solution)/shard_map/ppermute | solution.py:297
  17.9 0.0 collective-permute-start.4
  17.9 0.9 %collective-permute-start.3 = (f32[24,8,128]{2,1,0:T(8,128)}, f32[24,8,128]{2,1,0:T(8,128)S(1)}, u32[]{:S(2)}, u32[]{:S(2)}) collective-permute-start(f32[24,8,128]{2,1,0:T(8,128)} %shard_map.96.refs_4_), channel_id=1, source_target_pairs={{0,8},{2,10},{4,12},{6,14},{8,0},{10,2},{12,4},{14,6},{16,24},{18,... | collective-permute-start | bytes 294920 | tf_op jit(solution)/shard_map/ppermute | solution.py:297
  18.8 3.3 %collective-permute-done.5.refs_7_ = f32[24,8,128]{2,1,0:T(8,128)S(1)} collective-permute-done((f32[24,8,128]{2,1,0:T(8,128)}, f32[24,8,128]{2,1,0:T(8,128)S(1)}, u32[]{:S(2)}, u32[]{:S(2)}) %collective-permute-start.5) | collective-permute-done | bytes 98336 | tf_op jit(solution)/shard_map/ppermute | solution.py:297
  22.1 0.0 copy-start.3
  22.1 4.9 %collective-permute-done.4.refs_6_ = f32[24,8,128]{2,1,0:T(8,128)S(1)} collective-permute-done((f32[24,8,128]{2,1,0:T(8,128)}, f32[24,8,128]{2,1,0:T(8,128)S(1)}, u32[]{:S(2)}, u32[]{:S(2)}) %collective-permute-start.4) | collective-permute-done | bytes 98336 | tf_op jit(solution)/shard_map/ppermute | solution.py:297
  27.0 0.0 copy-start.4
  27.0 0.0 collective-permute-done.3.refs_5_
  27.0 0.0 copy-start.5
  27.0 0.0 copy-done.3
  27.0 0.6 %copy-done.4 = f32[24,8,128]{2,1,0:T(8,128)} copy-done((f32[24,8,128]{2,1,0:T(8,128)}, f32[24,8,128]{2,1,0:T(8,128)S(1)}, u32[]{:S(2)}) %copy-start.4) | copy-done | bytes 98328
  27.6 0.0 copy-done.5
  27.7 2.6 %shard_map.97 = (f32[16,512]{1,0:T(8,128)}, f32[16,512]{1,0:T(8,128)}, f32[2,16,512]{2,1,0:T(8,128)}) custom-call(s32[1]{0:T(128)} %bitcast.here_ref, s32[1]{0:T(128)} %bitcast.1.group_ref, s32[16]{0:T(128)} %length_ref.3, s32[4]{0:T(128)} %energy_ref.3, s32[4]{0:T(128)} %code_ref.1, f32[24,8,128]{2,1,0:T(8,128)} %shard_map.95.refs_0_, ...), custom_call_target="tpu_custom_call" | custom-call | tf_op jit(solution)/shard_map/pallas_call | solution.py:315
  30.3 1.5 %collective-permute-start.6 = (f32[2,16,512]{2,1,0:T(8,128)}, f32[2,16,512]{2,1,0:T(8,128)S(1)}, u32[]{:S(2)}, u32[]{:S(2)}) collective-permute-start(f32[2,16,512]{2,1,0:T(8,128)} %get-tuple-element.6), channel_id=1, source_target_pairs={{0,1},{1,0},{2,3},{3,2},{4,5},{5,4},{6,7},{7,6},{8,9},{9,8},{10,11... | collective-permute-start | bytes 196616 | tf_op jit(solution)/shard_map/ppermute | solution.py:332
  31.8 3.0 %collective-permute-done.6 = f32[2,16,512]{2,1,0:T(8,128)S(1)} collective-permute-done((f32[2,16,512]{2,1,0:T(8,128)}, f32[2,16,512]{2,1,0:T(8,128)S(1)}, u32[]{:S(2)}, u32[]{:S(2)}) %collective-permute-start.6) | collective-permute-done | bytes 65568 | tf_op jit(solution)/shard_map/ppermute | solution.py:332
  34.7 1.4 %fusion = (f32[16,512]{1,0:T(8,128)}, f32[16,512]{1,0:T(8,128)}) fusion(f32[16,512]{1,0:T(8,128)} %get-tuple-element.7, f32[2,16,512]{2,1,0:T(8,128)S(1)} %collective-permute-done.6, f32[16,512]{1,0:T(8,128)} %get-tuple-element.5), kind=kLoop, calls=%fused_computation.1 | loop fusion | flops 16384 | bytes 196608 | tf_op jit(solution)/shard_map/add | solution.py:333
Async XLA Ops:
  2.4 6.8 %collective-permute-start.2 = (f32[24,8,128]{2,1,0:T(8,128)}, f32[24,8,128]{2,1,0:T(8,128)S(1)}, u32[]{:S(2)}, u32[]{:S(2)}) collective-permute-start(f32[24,8,128]{2,1,0:T(8,128)} %shard_map.95.refs_0_), channel_id=1, source_target_pairs={{0,6},{2,4},{4,2},{6,0},{8,14},{10,12},{12,10},{14,8},{16,22},{18,... | collective-permute-start | bytes 294920 | tf_op jit(solution)/shard_map/ppermute | solution.py:286
  5.6 5.7 %collective-permute-start.1 = (f32[24,8,128]{2,1,0:T(8,128)}, f32[24,8,128]{2,1,0:T(8,128)S(1)}, u32[]{:S(2)}, u32[]{:S(2)}) collective-permute-start(f32[24,8,128]{2,1,0:T(8,128)} %shard_map.95.refs_0_), channel_id=1, source_target_pairs={{0,4},{2,6},{4,0},{6,2},{8,12},{10,14},{12,8},{14,10},{16,20},{18,... | collective-permute-start | bytes 294920 | tf_op jit(solution)/shard_map/ppermute | solution.py:286
  5.7 5.7 %collective-permute-start = (f32[24,8,128]{2,1,0:T(8,128)}, f32[24,8,128]{2,1,0:T(8,128)S(1)}, u32[]{:S(2)}, u32[]{:S(2)}) collective-permute-start(f32[24,8,128]{2,1,0:T(8,128)} %shard_map.95.refs_0_), channel_id=1, source_target_pairs={{0,2},{2,0},{4,6},{6,4},{8,10},{10,8},{12,14},{14,12},{16,18},{18,... | collective-permute-start | bytes 294920 | tf_op jit(solution)/shard_map/ppermute | solution.py:286
  9.1 2.2 %copy-start = (f32[24,8,128]{2,1,0:T(8,128)}, f32[24,8,128]{2,1,0:T(8,128)S(1)}, u32[]{:S(2)}) copy-start(f32[24,8,128]{2,1,0:T(8,128)S(1)} %collective-permute-done.2.refs_3_) | copy-start | bytes 294916
  11.3 0.6 %copy-start.1 = (f32[24,8,128]{2,1,0:T(8,128)}, f32[24,8,128]{2,1,0:T(8,128)S(1)}, u32[]{:S(2)}) copy-start(f32[24,8,128]{2,1,0:T(8,128)S(1)} %collective-permute-done.1.refs_2_) | copy-start | bytes 294916
  11.9 0.6 %copy-start.2 = (f32[24,8,128]{2,1,0:T(8,128)}, f32[24,8,128]{2,1,0:T(8,128)S(1)}, u32[]{:S(2)}) copy-start(f32[24,8,128]{2,1,0:T(8,128)S(1)} %collective-permute-done.refs_1_) | copy-start | bytes 294916
  14.4 7.7 %collective-permute-start.5 = (f32[24,8,128]{2,1,0:T(8,128)}, f32[24,8,128]{2,1,0:T(8,128)S(1)}, u32[]{:S(2)}, u32[]{:S(2)}) collective-permute-start(f32[24,8,128]{2,1,0:T(8,128)} %shard_map.96.refs_4_), channel_id=1, source_target_pairs={{0,24},{2,26},{4,28},{6,30},{8,16},{10,18},{12,20},{14,22},{16,8},... | collective-permute-start | bytes 294920 | tf_op jit(solution)/shard_map/ppermute | solution.py:297
  17.9 9.1 %collective-permute-start.4 = (f32[24,8,128]{2,1,0:T(8,128)}, f32[24,8,128]{2,1,0:T(8,128)S(1)}, u32[]{:S(2)}, u32[]{:S(2)}) collective-permute-start(f32[24,8,128]{2,1,0:T(8,128)} %shard_map.96.refs_4_), channel_id=1, source_target_pairs={{0,16},{2,18},{4,20},{6,22},{8,24},{10,26},{12,28},{14,30},{16,0},... | collective-permute-start | bytes 294920 | tf_op jit(solution)/shard_map/ppermute | solution.py:297
  17.9 9.1 %collective-permute-start.3 = (f32[24,8,128]{2,1,0:T(8,128)}, f32[24,8,128]{2,1,0:T(8,128)S(1)}, u32[]{:S(2)}, u32[]{:S(2)}) collective-permute-start(f32[24,8,128]{2,1,0:T(8,128)} %shard_map.96.refs_4_), channel_id=1, source_target_pairs={{0,8},{2,10},{4,12},{6,14},{8,0},{10,2},{12,4},{14,6},{16,24},{18,... | collective-permute-start | bytes 294920 | tf_op jit(solution)/shard_map/ppermute | solution.py:297
  22.1 4.9 %copy-start.3 = (f32[24,8,128]{2,1,0:T(8,128)}, f32[24,8,128]{2,1,0:T(8,128)S(1)}, u32[]{:S(2)}) copy-start(f32[24,8,128]{2,1,0:T(8,128)S(1)} %collective-permute-done.5.refs_7_) | copy-start | bytes 294916
  27.0 0.6 %copy-start.4 = (f32[24,8,128]{2,1,0:T(8,128)}, f32[24,8,128]{2,1,0:T(8,128)S(1)}, u32[]{:S(2)}) copy-start(f32[24,8,128]{2,1,0:T(8,128)S(1)} %collective-permute-done.4.refs_6_) | copy-start | bytes 294916
  27.0 0.7 %copy-start.5 = (f32[24,8,128]{2,1,0:T(8,128)}, f32[24,8,128]{2,1,0:T(8,128)S(1)}, u32[]{:S(2)}) copy-start(f32[24,8,128]{2,1,0:T(8,128)S(1)} %collective-permute-done.3.refs_5_) | copy-start | bytes 294916
  30.3 4.5 %collective-permute-start.6 = (f32[2,16,512]{2,1,0:T(8,128)}, f32[2,16,512]{2,1,0:T(8,128)S(1)}, u32[]{:S(2)}, u32[]{:S(2)}) collective-permute-start(f32[2,16,512]{2,1,0:T(8,128)} %get-tuple-element.6), channel_id=1, source_target_pairs={{0,1},{1,0},{2,3},{3,2},{4,5},{5,4},{6,7},{7,6},{8,9},{9,8},{10,11... | collective-permute-start | bytes 196616 | tf_op jit(solution)/shard_map/ppermute | solution.py:332

commit v6 on v3

--- a/solution.py
+++ b/solution.py
@@ -278,10 +278,11 @@
     mixed = devices & (devices - 1) == 0 and devices >= 4
     if mixed:
         size = 4
-        local = [packed] + [
-            lax.ppermute(packed, "slab", [(device, device ^ offset) for device in range(devices)])
-            for offset in range(1, size)
-        ]
+        def swap(value, offset):
+            return lax.ppermute(value, "slab", [(device, device ^ offset) for device in range(devices)])
+
+        across = swap(packed, 2)
+        local = [packed, swap(packed, 1), across, swap(across, 1)]
         summary = pl.pallas_call(
             group_kernel,
             out_shape=jax.ShapeDtypeStruct(packed.shape, jnp.float32),

time: 36.2 us -> 35.8 us (0.989)
  Pallas kernels: 6.5 us -> 7.91 us
  starting transfers between devices: 9.69 us -> 8.31 us
  local copies, waits for them, and re-layouts: 1.94 us -> 1.32 us
    ppermute x3, starting transfers between devices: 3.78 us -> 2.1 us  [swap(): lax.ppermute(value, 'slab', [(device, device ^ offset) for device in rang...]
    ppermute x3, waiting for transfers between devices: 7.72 us -> 8.87 us  [shards(): lax.ppermute(summary, 'slab', [(device, device ^ offset * size) for devic...]
    ppermute x3, waiting for transfers between devices: 4.99 us -> 4.22 us  [swap(): lax.ppermute(value, 'slab', [(device, device ^ offset) for device in rang...]
    pallas_call x1, Pallas kernels: 1.91 us -> 2.63 us  [shards(): pl.pallas_call(functools.partial(summary_kernel, slots=slots, points=poin...]
    pallas_call x1, Pallas kernels: 2.77 us -> 3.46 us  [shards(): pl.pallas_call(functools.partial(final_kernel, slots=slots, points=points...]
    unnamed x12, local copies, waits for them, and re-layouts: 1.94 us -> 1.32 us
where the time goes in v6:
time: 35.8 us; the launch traced here: 35.7 us
  waiting for transfers between devices  16 us (45%)
  starting transfers between devices  8.31 us (23%)
  Pallas kernels  7.91 us (22%)
  other arithmetic  1.41 us (4%)
  local copies, waits for them, and re-layouts  1.32 us (4%)
  between operations  0.66 us (2%)
    ppermute x3, waiting for transfers between devices, shards(): lax.ppermute(summary, 'slab', [(device, device ^ offset * size) for devic...  8.87 us
    ppermute x3, starting transfers between devices, shards(): lax.ppermute(summary, 'slab', [(device, device ^ offset * size) for devic...  4.69 us
    ppermute x3, waiting for transfers between devices, swap(): lax.ppermute(value, 'slab', [(device, device ^ offset) for device in rang...  4.22 us
    pallas_call x1, Pallas kernels, shards(): pl.pallas_call(functools.partial(final_kernel, slots=slots, points=points...  3.46 us
    ppermute x1, waiting for transfers between devices, shards(): theirs = lax.ppermute(theirs, 'energy', [(0, 1), (1, 0)])  2.96 us
    pallas_call x1, Pallas kernels, shards(): pl.pallas_call(functools.partial(summary_kernel, slots=slots, points=poin...  2.63 us
    ppermute x3, starting transfers between devices, swap(): lax.ppermute(value, 'slab', [(device, device ^ offset) for device in rang...  2.1 us
    pallas_call x1, Pallas kernels, shards(): pl.pallas_call(group_kernel, out_shape=jax.ShapeDtypeStruct(packed.shape,...  1.82 us
  transfers between devices with their start and end apart: 7, of which 5 were waited for; matrix products, arithmetic and copies ran while one was open for 0% of the time, Pallas kernels for 0%

profile of v6, /device:TPU:0, one launch (start us, length us, event | category | flops | bytes accessed | tf_op | source)
XLA Modules:
  0.0 35.7 jit_solution(12546209938688252729)
XLA Ops:
  0.6 2.6 %shard_map.95.refs_0_ = f32[24,8,128]{2,1,0:T(8,128)} custom-call(s32[1]{0:T(128)} %bitcast.here_ref, s32[16]{0:T(128)} %length_ref.3, s32[4]{0:T(128)} %energy_ref.3, f32[1,1024]{1,0:T(1,128)} %bitcast.11, f32[16,1024]{1,0:T(8,128)} %refs_9_.1, f32[16,1024]{1,0:T(8,128)} %refs_10_.1, f32[4,2,1024]{2,1,0:T(2,128)} %refs_11_.1, f32[4,2,1024]{2,1,0:T(2,128)} %refs_12_.1), custom_call_target="tpu_custom_call" | custom-call | tf_op jit(solution)/shard_map/pallas_call | solution.py:271
  3.3 2.1 %collective-permute-start.1 = (f32[24,8,128]{2,1,0:T(8,128)}, f32[24,8,128]{2,1,0:T(8,128)S(1)}, u32[]{:S(2)}, u32[]{:S(2)}) collective-permute-start(f32[24,8,128]{2,1,0:T(8,128)} %shard_map.95.refs_0_), channel_id=1, source_target_pairs={{0,4},{2,6},{4,0},{6,2},{8,12},{10,14},{12,8},{14,10},{16,20},{18,... | collective-permute-start | bytes 294920 | tf_op jit(solution)/shard_map/ppermute | solution.py:282
  5.4 0.0 collective-permute-start
  5.4 2.9 %collective-permute-done.1.refs_2_ = f32[24,8,128]{2,1,0:T(8,128)S(1)} collective-permute-done((f32[24,8,128]{2,1,0:T(8,128)}, f32[24,8,128]{2,1,0:T(8,128)S(1)}, u32[]{:S(2)}, u32[]{:S(2)}) %collective-permute-start.1) | collective-permute-done | bytes 98336 | tf_op jit(solution)/shard_map/ppermute | solution.py:282
  8.3 0.0 copy-start
  8.3 0.0 collective-permute-start.2
  8.3 0.0 collective-permute-done.refs_1_
  8.3 0.0 copy-start.1
  8.3 1.3 %collective-permute-done.2.refs_3_ = f32[24,8,128]{2,1,0:T(8,128)S(1)} collective-permute-done((f32[24,8,128]{2,1,0:T(8,128)S(1)}, f32[24,8,128]{2,1,0:T(8,128)S(1)}, u32[]{:S(2)}, u32[]{:S(2)}) %collective-permute-start.2) | collective-permute-done | bytes 98336 | tf_op jit(solution)/shard_map/ppermute | solution.py:282
  9.6 0.0 copy-done
  9.6 0.0 copy-done.1
  9.6 0.0 copy-start.2
  9.6 0.6 %copy-done.2 = f32[24,8,128]{2,1,0:T(8,128)} copy-done((f32[24,8,128]{2,1,0:T(8,128)}, f32[24,8,128]{2,1,0:T(8,128)S(1)}, u32[]{:S(2)}) %copy-start.2) | copy-done | bytes 98328
  10.3 1.8 %shard_map.96.refs_4_ = f32[24,8,128]{2,1,0:T(8,128)} custom-call(s32[1]{0:T(128)} %bitcast.here_ref, f32[24,8,128]{2,1,0:T(8,128)} %shard_map.95.refs_0_, f32[24,8,128]{2,1,0:T(8,128)} %copy-done.1, f32[24,8,128]{2,1,0:T(8,128)} %copy-done, f32[24,8,128]{2,1,0:T(8,128)} %copy-done.2), custom_call_target="tpu_custom_call" | custom-call | tf_op jit(solution)/shard_map/pallas_call | solution.py:286
  12.1 4.1 %collective-permute-start.5 = (f32[24,8,128]{2,1,0:T(8,128)}, f32[24,8,128]{2,1,0:T(8,128)S(1)}, u32[]{:S(2)}, u32[]{:S(2)}) collective-permute-start(f32[24,8,128]{2,1,0:T(8,128)} %shard_map.96.refs_4_), channel_id=1, source_target_pairs={{0,24},{2,26},{4,28},{6,30},{8,16},{10,18},{12,20},{14,22},{16,8},... | collective-permute-start | bytes 294920 | tf_op jit(solution)/shard_map/ppermute | solution.py:294
  16.2 0.1 collective-permute-start.4
  16.3 0.5 %collective-permute-start.3 = (f32[24,8,128]{2,1,0:T(8,128)}, f32[24,8,128]{2,1,0:T(8,128)S(1)}, u32[]{:S(2)}, u32[]{:S(2)}) collective-permute-start(f32[24,8,128]{2,1,0:T(8,128)} %shard_map.96.refs_4_), channel_id=1, source_target_pairs={{0,8},{2,10},{4,12},{6,14},{8,0},{10,2},{12,4},{14,6},{16,24},{18,... | collective-permute-start | bytes 294920 | tf_op jit(solution)/shard_map/ppermute | solution.py:294
  16.8 3.3 %collective-permute-done.5.refs_7_ = f32[24,8,128]{2,1,0:T(8,128)S(1)} collective-permute-done((f32[24,8,128]{2,1,0:T(8,128)}, f32[24,8,128]{2,1,0:T(8,128)S(1)}, u32[]{:S(2)}, u32[]{:S(2)}) %collective-permute-start.5) | collective-permute-done | bytes 98336 | tf_op jit(solution)/shard_map/ppermute | solution.py:294
  20.1 0.0 copy-start.3
  20.1 5.5 %collective-permute-done.4.refs_6_ = f32[24,8,128]{2,1,0:T(8,128)S(1)} collective-permute-done((f32[24,8,128]{2,1,0:T(8,128)}, f32[24,8,128]{2,1,0:T(8,128)S(1)}, u32[]{:S(2)}, u32[]{:S(2)}) %collective-permute-start.4) | collective-permute-done | bytes 98336 | tf_op jit(solution)/shard_map/ppermute | solution.py:294
  25.6 0.0 copy-start.4
  25.6 0.0 collective-permute-done.3.refs_5_
  25.6 0.0 copy-start.5
  25.6 0.0 copy-done.3
  25.6 0.6 %copy-done.4 = f32[24,8,128]{2,1,0:T(8,128)} copy-done((f32[24,8,128]{2,1,0:T(8,128)}, f32[24,8,128]{2,1,0:T(8,128)S(1)}, u32[]{:S(2)}) %copy-start.4) | copy-done | bytes 98328
  26.3 0.0 copy-done.5
  26.3 3.5 %shard_map.97 = (f32[16,512]{1,0:T(8,128)}, f32[16,512]{1,0:T(8,128)}, f32[2,16,512]{2,1,0:T(8,128)}) custom-call(s32[1]{0:T(128)} %bitcast.here_ref, s32[1]{0:T(128)} %bitcast.1.group_ref, s32[16]{0:T(128)} %length_ref.3, s32[4]{0:T(128)} %energy_ref.3, s32[4]{0:T(128)} %code_ref.1, f32[24,8,128]{2,1,0:T(8,128)} %shard_map.95.refs_0_, ...), custom_call_target="tpu_custom_call" | custom-call | tf_op jit(solution)/shard_map/pallas_call | solution.py:312
  29.8 1.5 %collective-permute-start.6 = (f32[2,16,512]{2,1,0:T(8,128)}, f32[2,16,512]{2,1,0:T(8,128)S(1)}, u32[]{:S(2)}, u32[]{:S(2)}) collective-permute-start(f32[2,16,512]{2,1,0:T(8,128)} %get-tuple-element.6), channel_id=1, source_target_pairs={{0,1},{1,0},{2,3},{3,2},{4,5},{5,4},{6,7},{7,6},{8,9},{9,8},{10,11... | collective-permute-start | bytes 196616 | tf_op jit(solution)/shard_map/ppermute | solution.py:329
  31.3 3.0 %collective-permute-done.6 = f32[2,16,512]{2,1,0:T(8,128)S(1)} collective-permute-done((f32[2,16,512]{2,1,0:T(8,128)}, f32[2,16,512]{2,1,0:T(8,128)S(1)}, u32[]{:S(2)}, u32[]{:S(2)}) %collective-permute-start.6) | collective-permute-done | bytes 65568 | tf_op jit(solution)/shard_map/ppermute | solution.py:329
  34.2 1.4 %fusion = (f32[16,512]{1,0:T(8,128)}, f32[16,512]{1,0:T(8,128)}) fusion(f32[16,512]{1,0:T(8,128)} %get-tuple-element.7, f32[2,16,512]{2,1,0:T(8,128)S(1)} %collective-permute-done.6, f32[16,512]{1,0:T(8,128)} %get-tuple-element.5), kind=kLoop, calls=%fused_computation.1 | loop fusion | flops 16384 | bytes 196608 | tf_op jit(solution)/shard_map/add | solution.py:330
Async XLA Ops:
  3.3 5.0 %collective-permute-start.1 = (f32[24,8,128]{2,1,0:T(8,128)}, f32[24,8,128]{2,1,0:T(8,128)S(1)}, u32[]{:S(2)}, u32[]{:S(2)}) collective-permute-start(f32[24,8,128]{2,1,0:T(8,128)} %shard_map.95.refs_0_), channel_id=1, source_target_pairs={{0,4},{2,6},{4,0},{6,2},{8,12},{10,14},{12,8},{14,10},{16,20},{18,... | collective-permute-start | bytes 294920 | tf_op jit(solution)/shard_map/ppermute | solution.py:282
  5.4 2.9 %collective-permute-start = (f32[24,8,128]{2,1,0:T(8,128)}, f32[24,8,128]{2,1,0:T(8,128)S(1)}, u32[]{:S(2)}, u32[]{:S(2)}) collective-permute-start(f32[24,8,128]{2,1,0:T(8,128)} %shard_map.95.refs_0_), channel_id=1, source_target_pairs={{0,2},{2,0},{4,6},{6,4},{8,10},{10,8},{12,14},{14,12},{16,18},{18,... | collective-permute-start | bytes 294920 | tf_op jit(solution)/shard_map/ppermute | solution.py:282
  8.3 1.3 %copy-start = (f32[24,8,128]{2,1,0:T(8,128)}, f32[24,8,128]{2,1,0:T(8,128)S(1)}, u32[]{:S(2)}) copy-start(f32[24,8,128]{2,1,0:T(8,128)S(1)} %collective-permute-done.1.refs_2_) | copy-start | bytes 294916
  8.3 1.3 %collective-permute-start.2 = (f32[24,8,128]{2,1,0:T(8,128)S(1)}, f32[24,8,128]{2,1,0:T(8,128)S(1)}, u32[]{:S(2)}, u32[]{:S(2)}) collective-permute-start(f32[24,8,128]{2,1,0:T(8,128)S(1)} %collective-permute-done.1.refs_2_), channel_id=1, source_target_pairs={{0,2},{2,0},{4,6},{6,4},{8,10},{10,8},{12,14},{14,12},{16,18},{18,... | collective-permute-start | bytes 294920 | tf_op jit(solution)/shard_map/ppermute | solution.py:282
  8.3 1.3 %copy-start.1 = (f32[24,8,128]{2,1,0:T(8,128)}, f32[24,8,128]{2,1,0:T(8,128)S(1)}, u32[]{:S(2)}) copy-start(f32[24,8,128]{2,1,0:T(8,128)S(1)} %collective-permute-done.refs_1_) | copy-start | bytes 294916
  9.6 0.6 %copy-start.2 = (f32[24,8,128]{2,1,0:T(8,128)}, f32[24,8,128]{2,1,0:T(8,128)S(1)}, u32[]{:S(2)}) copy-start(f32[24,8,128]{2,1,0:T(8,128)S(1)} %collective-permute-done.2.refs_3_) | copy-start | bytes 294916
  12.1 8.0 %collective-permute-start.5 = (f32[24,8,128]{2,1,0:T(8,128)}, f32[24,8,128]{2,1,0:T(8,128)S(1)}, u32[]{:S(2)}, u32[]{:S(2)}) collective-permute-start(f32[24,8,128]{2,1,0:T(8,128)} %shard_map.96.refs_4_), channel_id=1, source_target_pairs={{0,24},{2,26},{4,28},{6,30},{8,16},{10,18},{12,20},{14,22},{16,8},... | collective-permute-start | bytes 294920 | tf_op jit(solution)/shard_map/ppermute | solution.py:294
  16.2 9.4 %collective-permute-start.4 = (f32[24,8,128]{2,1,0:T(8,128)}, f32[24,8,128]{2,1,0:T(8,128)S(1)}, u32[]{:S(2)}, u32[]{:S(2)}) collective-permute-start(f32[24,8,128]{2,1,0:T(8,128)} %shard_map.96.refs_4_), channel_id=1, source_target_pairs={{0,16},{2,18},{4,20},{6,22},{8,24},{10,26},{12,28},{14,30},{16,0},... | collective-permute-start | bytes 294920 | tf_op jit(solution)/shard_map/ppermute | solution.py:294
  16.3 9.4 %collective-permute-start.3 = (f32[24,8,128]{2,1,0:T(8,128)}, f32[24,8,128]{2,1,0:T(8,128)S(1)}, u32[]{:S(2)}, u32[]{:S(2)}) collective-permute-start(f32[24,8,128]{2,1,0:T(8,128)} %shard_map.96.refs_4_), channel_id=1, source_target_pairs={{0,8},{2,10},{4,12},{6,14},{8,0},{10,2},{12,4},{14,6},{16,24},{18,... | collective-permute-start | bytes 294920 | tf_op jit(solution)/shard_map/ppermute | solution.py:294
  20.1 5.6 %copy-start.3 = (f32[24,8,128]{2,1,0:T(8,128)}, f32[24,8,128]{2,1,0:T(8,128)S(1)}, u32[]{:S(2)}) copy-start(f32[24,8,128]{2,1,0:T(8,128)S(1)} %collective-permute-done.5.refs_7_) | copy-start | bytes 294916
  25.6 0.6 %copy-start.4 = (f32[24,8,128]{2,1,0:T(8,128)}, f32[24,8,128]{2,1,0:T(8,128)S(1)}, u32[]{:S(2)}) copy-start(f32[24,8,128]{2,1,0:T(8,128)S(1)} %collective-permute-done.4.refs_6_) | copy-start | bytes 294916
  25.6 0.7 %copy-start.5 = (f32[24,8,128]{2,1,0:T(8,128)}, f32[24,8,128]{2,1,0:T(8,128)S(1)}, u32[]{:S(2)}) copy-start(f32[24,8,128]{2,1,0:T(8,128)S(1)} %collective-permute-done.3.refs_5_) | copy-start | bytes 294916
  29.8 4.5 %collective-permute-start.6 = (f32[2,16,512]{2,1,0:T(8,128)}, f32[2,16,512]{2,1,0:T(8,128)S(1)}, u32[]{:S(2)}, u32[]{:S(2)}) collective-permute-start(f32[2,16,512]{2,1,0:T(8,128)} %get-tuple-element.6), channel_id=1, source_target_pairs={{0,1},{1,0},{2,3},{3,2},{4,5},{5,4},{6,7},{7,6},{8,9},{9,8},{10,11... | collective-permute-start | bytes 196616 | tf_op jit(solution)/shard_map/ppermute | solution.py:329

commit v7 on v6

--- a/solution.py
+++ b/solution.py
@@ -122,15 +122,16 @@
     return (left[0] + f_re, left[1] + f_im, right[2] + g_re, right[3] + g_im, x_re, x_im)
 
 
-def in_order(refs, own, mixed):
-    loaded = [ref[...] for ref in refs]
+def in_order(refs, own, mixed, loaded=None):
+    if loaded is None:
+        loaded = [ref[...] for ref in refs]
     if not mixed:
         return loaded
     ordered = []
-    for position in range(len(refs)):
+    for position in range(len(loaded)):
         offset = jnp.bitwise_xor(own, position)
         value = loaded[0]
-        for index in range(1, len(refs)):
+        for index in range(1, len(loaded)):
             value = jnp.where(offset == index, loaded[index], value)
         ordered.append(value)
     return ordered
@@ -154,11 +155,11 @@
 
 
 def final_kernel(here_ref, group_ref, length_ref, energy_ref, code_ref, *refs,
-                 slots, points, devices, mixed, size, groups, scale):
+                 slots, points, devices, mixed, size, groups, scale, relay):
     local_refs = refs[:size]
-    group_refs = refs[size:size + groups]
+    group_refs = refs[size:size + groups + 2 * relay]
     (floor_ref, noise_ref, hop_ref, shift_ref, width_ref, dens_out_ref, bond_out_ref, theirs_ref,
-     left_re_ref, left_im_ref, dens_ref, bond_ref, table_ref) = refs[size + groups:]
+     left_re_ref, left_im_ref, dens_ref, bond_ref, table_ref) = refs[size + groups + 2 * relay:]
     build_table(floor_ref, noise_ref, hop_ref, shift_ref, width_ref, table_ref)
     here = here_ref[0]
     count = length_ref[here]
@@ -186,7 +187,19 @@
         return tuple(jnp.where(keep, n, o) for n, o in zip(new, old))
 
     zero = jnp.zeros((points,) + table_ref.shape[1:], jnp.float32)
-    group_blocks = [split_fields(v, points) for v in in_order(group_refs, group_here, mixed)]
+    group_values = None
+    if relay:
+        own_g, near, far, back, swapped, swapped_far = [ref[...] for ref in group_refs]
+        first_core = jnp.bitwise_and(here, 1) == 0
+        group_values = [
+            own_g,
+            jnp.where(first_core, near, swapped),
+            jnp.where(first_core, far, swapped_far),
+            jnp.where(first_core, swapped, back),
+        ]
+    group_blocks = [
+        split_fields(v, points) for v in in_order(group_refs, group_here, mixed, group_values)
+    ]
     local_blocks = [split_fields(v, points) for v in in_order(local_refs, member_here, mixed)]
     into = (zero, zero)
     for group in range(groups):
@@ -276,6 +289,7 @@
         scratch_shapes=[pltpu.VMEM(table_shape, jnp.float32)],
     )(here_arr, lengths, energy_index, *raw)
     mixed = devices & (devices - 1) == 0 and devices >= 4
+    relay = False
     if mixed:
         size = 4
         def swap(value, offset):
@@ -290,10 +304,15 @@
             out_specs=vmem,
         )(here_arr, *local)
         if devices == size * size:
-            every = [summary] + [
-                lax.ppermute(summary, "slab", [(device, device ^ (offset * size)) for device in range(devices)])
-                for offset in range(1, size)
-            ]
+            def fetch(offset, core):
+                pairs = [(device, device ^ offset) for device in range(devices) if device % 2 == core]
+                return lax.ppermute(summary, "slab", pairs)
+
+            near, far, back = fetch(size, 0), fetch(2 * size, 0), fetch(3 * size, 1)
+            swapped = swap(near + back, 1)
+            swapped_far = swap(far, 1)
+            every = [summary, near, far, back, swapped, swapped_far]
+            relay = True
         else:
             stacked = summary[None]
             distance = size
@@ -312,7 +331,8 @@
     density, bond_density, theirs = pl.pallas_call(
         functools.partial(
             final_kernel, slots=slots, points=points, devices=devices, mixed=mixed,
-            size=len(local), groups=len(every), scale=1.0 / (32.0 * points * groups),
+            size=len(local), groups=len(every) - 2 * relay, relay=relay,
+            scale=1.0 / (32.0 * points * groups),
         ),
         out_shape=(half, half, jax.ShapeDtypeStruct((2, slots, modes // 2), jnp.float32)),
         in_specs=[smem] * 5 + [vmem] * (len(local) + len(every) + len(raw)),

time: 35.8 us -> 36.9 us (1.031)
  starting transfers between devices: 8.31 us -> 12.4 us
  waiting for transfers between devices: 16 us -> 12.8 us
  local copies, waits for them, and re-layouts: 1.32 us -> 1.89 us
    ppermute x3, waiting for transfers between devices: 8.87 us -> 3.79 us  [fetch(): return lax.ppermute(summary, 'slab', pairs)]
    ppermute x3, starting transfers between devices: 4.69 us -> 8.31 us  [fetch(): return lax.ppermute(summary, 'slab', pairs)]
    ppermute x3 -> x5, waiting for transfers between devices: 4.22 us -> 6.02 us  [swap(): lax.ppermute(value, 'slab', [(device, device ^ offset) for device in rang...]
    unnamed x12 -> x16, local copies, waits for them, and re-layouts: 1.32 us -> 1.89 us
    ppermute x3 -> x5, starting transfers between devices: 2.1 us -> 2.56 us  [swap(): lax.ppermute(value, 'slab', [(device, device ^ offset) for device in rang...]
  transfers between devices with their start and end apart: 7 -> 9, of which waited for: 5 -> 6; matrix products, arithmetic and copies ran while one was open for 0% -> 0% of each run, Pallas kernels for 0% -> 0%
where the time goes in v7:
time: 36.9 us; the launch traced here: 37.1 us
  waiting for transfers between devices  12.8 us (35%)
  starting transfers between devices  12.4 us (34%)
  Pallas kernels  7.89 us (21%)
  local copies, waits for them, and re-layouts  1.89 us (5%)
  other arithmetic  1.42 us (4%)
  between operations  0.72 us (2%)
    ppermute x3, starting transfers between devices, fetch(): return lax.ppermute(summary, 'slab', pairs)  8.31 us
    ppermute x5, waiting for transfers between devices, swap(): lax.ppermute(value, 'slab', [(device, device ^ offset) for device in rang...  6.02 us
    ppermute x3, waiting for transfers between devices, fetch(): return lax.ppermute(summary, 'slab', pairs)  3.79 us
    pallas_call x1, Pallas kernels, shards(): pl.pallas_call(functools.partial(final_kernel, slots=slots, points=points...  3.48 us
    ppermute x1, waiting for transfers between devices, shards(): theirs = lax.ppermute(theirs, 'energy', [(0, 1), (1, 0)])  2.96 us
    pallas_call x1, Pallas kernels, shards(): pl.pallas_call(functools.partial(summary_kernel, slots=slots, points=poin...  2.59 us
    ppermute x5, starting transfers between devices, swap(): lax.ppermute(value, 'slab', [(device, device ^ offset) for device in rang...  2.56 us
    unnamed x16, local copies, waits for them, and re-layouts  1.89 us
  transfers between devices with their start and end apart: 9, of which 6 were waited for; matrix products, arithmetic and copies ran while one was open for 0% of the time, Pallas kernels for 0%

profile of v7, /device:TPU:0, one launch (start us, length us, event | category | flops | bytes accessed | tf_op | source)
XLA Modules:
  0.0 37.1 jit_solution(3142447246741942618)
XLA Ops:
  0.6 2.6 %shard_map.95.refs_0_ = f32[24,8,128]{2,1,0:T(8,128)} custom-call(s32[1]{0:T(128)} %bitcast.here_ref, s32[16]{0:T(128)} %length_ref.3, s32[4]{0:T(128)} %energy_ref.3, f32[1,1024]{1,0:T(1,128)} %bitcast.11, f32[16,1024]{1,0:T(8,128)} %refs_11_.1, f32[16,1024]{1,0:T(8,128)} %refs_12_.1, f32[4,2,1024]{2,1,0:T(2,128)} %refs_13_.1, f32[4,2,1024]{2,1,0:T(2,128)} %refs_14_.1), custom_call_target="tpu_custom_call" | custom-call | tf_op jit(solution)/shard_map/pallas_call | solution.py:284
  3.2 2.5 %collective-permute-start.1 = (f32[24,8,128]{2,1,0:T(8,128)}, f32[24,8,128]{2,1,0:T(8,128)S(1)}, u32[]{:S(2)}, u32[]{:S(2)}) collective-permute-start(f32[24,8,128]{2,1,0:T(8,128)} %shard_map.95.refs_0_), channel_id=1, source_target_pairs={{0,4},{2,6},{4,0},{6,2},{8,12},{10,14},{12,8},{14,10},{16,20},{18,... | collective-permute-start | bytes 294920 | tf_op jit(solution)/shard_map/ppermute | solution.py:296
  5.7 0.1 collective-permute-start
  5.8 3.4 %collective-permute-done.1.refs_2_ = f32[24,8,128]{2,1,0:T(8,128)S(1)} collective-permute-done((f32[24,8,128]{2,1,0:T(8,128)}, f32[24,8,128]{2,1,0:T(8,128)S(1)}, u32[]{:S(2)}, u32[]{:S(2)}) %collective-permute-start.1) | collective-permute-done | bytes 98336 | tf_op jit(solution)/shard_map/ppermute | solution.py:296
  9.2 0.0 collective-permute-start.2
  9.2 0.0 collective-permute-done.refs_1_
  9.2 0.0 copy-start.1
  9.2 1.3 %collective-permute-done.2.refs_3_ = f32[24,8,128]{2,1,0:T(8,128)S(1)} collective-permute-done((f32[24,8,128]{2,1,0:T(8,128)S(1)}, f32[24,8,128]{2,1,0:T(8,128)S(1)}, u32[]{:S(2)}, u32[]{:S(2)}) %collective-permute-start.2) | collective-permute-done | bytes 98336 | tf_op jit(solution)/shard_map/ppermute | solution.py:296
  10.5 0.0 copy-done
  10.5 0.0 copy-done.1
  10.5 0.6 %copy-done.2 = f32[24,8,128]{2,1,0:T(8,128)} copy-done((f32[24,8,128]{2,1,0:T(8,128)}, f32[24,8,128]{2,1,0:T(8,128)S(1)}, u32[]{:S(2)}) %copy-start.2) | copy-done | bytes 98328
  11.2 1.8 %shard_map.96.refs_4_ = f32[24,8,128]{2,1,0:T(8,128)} custom-call(s32[1]{0:T(128)} %bitcast.here_ref, f32[24,8,128]{2,1,0:T(8,128)} %shard_map.95.refs_0_, f32[24,8,128]{2,1,0:T(8,128)} %copy-done.1, f32[24,8,128]{2,1,0:T(8,128)} %copy-done, f32[24,8,128]{2,1,0:T(8,128)} %copy-done.2), custom_call_target="tpu_custom_call" | custom-call | tf_op jit(solution)/shard_map/pallas_call | solution.py:300
  13.0 4.7 %collective-permute-start.4 = (f32[24,8,128]{2,1,0:T(8,128)}, f32[24,8,128]{2,1,0:T(8,128)S(1)}, u32[]{:S(2)}, u32[]{:S(2)}) collective-permute-start(f32[24,8,128]{2,1,0:T(8,128)} %shard_map.96.refs_4_), channel_id=1, source_target_pairs={{0,16},{4,20},{8,24},{12,28},{16,0},{20,4},{24,8},{28,12},{1,17},{... | collective-permute-start | bytes 294920 | tf_op jit(solution)/shard_map/ppermute | solution.py:309
  17.7 0.7 %collective-permute-start.5 = (f32[24,8,128]{2,1,0:T(8,128)}, f32[24,8,128]{2,1,0:T(8,128)S(1)}, u32[]{:S(2)}, u32[]{:S(2)}) collective-permute-start(f32[24,8,128]{2,1,0:T(8,128)} %shard_map.96.refs_4_), channel_id=1, source_target_pairs={{2,26},{6,30},{10,18},{14,22},{18,10},{22,14},{26,2},{30,6},{3,27}... | collective-permute-start | bytes 294920 | tf_op jit(solution)/shard_map/ppermute | solution.py:309
  18.4 2.9 %collective-permute-start.3 = (f32[24,8,128]{2,1,0:T(8,128)}, f32[24,8,128]{2,1,0:T(8,128)S(1)}, u32[]{:S(2)}, u32[]{:S(2)}) collective-permute-start(f32[24,8,128]{2,1,0:T(8,128)} %shard_map.96.refs_4_), channel_id=1, source_target_pairs={{0,8},{4,12},{8,0},{12,4},{16,24},{20,28},{24,16},{28,20},{1,9},{5... | collective-permute-start | bytes 294920 | tf_op jit(solution)/shard_map/ppermute | solution.py:309
  21.3 2.2 %collective-permute-done.4.refs_6_ = f32[24,8,128]{2,1,0:T(8,128)S(1)} collective-permute-done((f32[24,8,128]{2,1,0:T(8,128)}, f32[24,8,128]{2,1,0:T(8,128)S(1)}, u32[]{:S(2)}, u32[]{:S(2)}) %collective-permute-start.4) | collective-permute-done | bytes 98336 | tf_op jit(solution)/shard_map/ppermute | solution.py:309
  23.5 0.0 collective-permute-start.7
  23.5 0.0 collective-permute-done.5.refs_7_
  23.6 0.0 copy-start.3
  23.6 1.6 %collective-permute-done.3.refs_5_ = f32[24,8,128]{2,1,0:T(8,128)S(1)} collective-permute-done((f32[24,8,128]{2,1,0:T(8,128)}, f32[24,8,128]{2,1,0:T(8,128)S(1)}, u32[]{:S(2)}, u32[]{:S(2)}) %collective-permute-start.3) | collective-permute-done | bytes 98336 | tf_op jit(solution)/shard_map/ppermute | solution.py:309
  25.2 0.0 copy-done.5
  25.2 0.0 copy-done.3
  25.2 0.6 %copy-done.4 = f32[24,8,128]{2,1,0:T(8,128)} copy-done((f32[24,8,128]{2,1,0:T(8,128)}, f32[24,8,128]{2,1,0:T(8,128)S(1)}, u32[]{:S(2)}) %copy-start.4) | copy-done | bytes 98328
  25.8 0.0 collective-permute-start.6
  25.8 0.0 collective-permute-done.7.refs_9_
  25.8 1.3 %collective-permute-done.6.refs_8_ = f32[24,8,128]{2,1,0:T(8,128)S(1)} collective-permute-done((f32[24,8,128]{2,1,0:T(8,128)S(1)}, f32[24,8,128]{2,1,0:T(8,128)S(1)}, u32[]{:S(2)}, u32[]{:S(2)}) %collective-permute-start.6) | collective-permute-done | bytes 98336 | tf_op jit(solution)/shard_map/ppermute | solution.py:296
  27.1 0.0 copy-done.6
  27.1 0.6 %copy-done.7 = f32[24,8,128]{2,1,0:T(8,128)} copy-done((f32[24,8,128]{2,1,0:T(8,128)}, f32[24,8,128]{2,1,0:T(8,128)S(1)}, u32[]{:S(2)}) %copy-start.7) | copy-done | bytes 98328
  27.7 3.5 %shard_map.97 = (f32[16,512]{1,0:T(8,128)}, f32[16,512]{1,0:T(8,128)}, f32[2,16,512]{2,1,0:T(8,128)}) custom-call(s32[1]{0:T(128)} %bitcast.here_ref, s32[1]{0:T(128)} %bitcast.1.group_ref, s32[16]{0:T(128)} %length_ref.3, s32[4]{0:T(128)} %energy_ref.3, s32[4]{0:T(128)} %code_ref.1, f32[24,8,128]{2,1,0:T(8,128)} %shard_map.95.refs_0_, ...), custom_call_target="tpu_custom_call" | custom-call | tf_op jit(solution)/shard_map/pallas_call | solution.py:331
  31.2 1.5 %collective-permute-start.8 = (f32[2,16,512]{2,1,0:T(8,128)}, f32[2,16,512]{2,1,0:T(8,128)S(1)}, u32[]{:S(2)}, u32[]{:S(2)}) collective-permute-start(f32[2,16,512]{2,1,0:T(8,128)} %get-tuple-element.6), channel_id=1, source_target_pairs={{0,1},{1,0},{2,3},{3,2},{4,5},{5,4},{6,7},{7,6},{8,9},{9,8},{10,11... | collective-permute-start | bytes 196616 | tf_op jit(solution)/shard_map/ppermute | solution.py:349
  32.7 3.0 %collective-permute-done.8 = f32[2,16,512]{2,1,0:T(8,128)S(1)} collective-permute-done((f32[2,16,512]{2,1,0:T(8,128)}, f32[2,16,512]{2,1,0:T(8,128)S(1)}, u32[]{:S(2)}, u32[]{:S(2)}) %collective-permute-start.8) | collective-permute-done | bytes 65568 | tf_op jit(solution)/shard_map/ppermute | solution.py:349
  35.7 1.4 %fusion = (f32[16,512]{1,0:T(8,128)}, f32[16,512]{1,0:T(8,128)}) fusion(f32[16,512]{1,0:T(8,128)} %get-tuple-element.7, f32[2,16,512]{2,1,0:T(8,128)S(1)} %collective-permute-done.8, f32[16,512]{1,0:T(8,128)} %get-tuple-element.5), kind=kLoop, calls=%fused_computation.1 | loop fusion | flops 16384 | bytes 196608 | tf_op jit(solution)/shard_map/add | solution.py:350
  (7 shorter events, 0.0 us)
Async XLA Ops:
  3.2 6.0 %collective-permute-start.1 = (f32[24,8,128]{2,1,0:T(8,128)}, f32[24,8,128]{2,1,0:T(8,128)S(1)}, u32[]{:S(2)}, u32[]{:S(2)}) collective-permute-start(f32[24,8,128]{2,1,0:T(8,128)} %shard_map.95.refs_0_), channel_id=1, source_target_pairs={{0,4},{2,6},{4,0},{6,2},{8,12},{10,14},{12,8},{14,10},{16,20},{18,... | collective-permute-start | bytes 294920 | tf_op jit(solution)/shard_map/ppermute | solution.py:296
  5.7 3.5 %collective-permute-start = (f32[24,8,128]{2,1,0:T(8,128)}, f32[24,8,128]{2,1,0:T(8,128)S(1)}, u32[]{:S(2)}, u32[]{:S(2)}) collective-permute-start(f32[24,8,128]{2,1,0:T(8,128)} %shard_map.95.refs_0_), channel_id=1, source_target_pairs={{0,2},{2,0},{4,6},{6,4},{8,10},{10,8},{12,14},{14,12},{16,18},{18,... | collective-permute-start | bytes 294920 | tf_op jit(solution)/shard_map/ppermute | solution.py:296
  9.2 1.3 %copy-start = (f32[24,8,128]{2,1,0:T(8,128)}, f32[24,8,128]{2,1,0:T(8,128)S(1)}, u32[]{:S(2)}) copy-start(f32[24,8,128]{2,1,0:T(8,128)S(1)} %collective-permute-done.1.refs_2_) | copy-start | bytes 294916
  9.2 1.3 %collective-permute-start.2 = (f32[24,8,128]{2,1,0:T(8,128)S(1)}, f32[24,8,128]{2,1,0:T(8,128)S(1)}, u32[]{:S(2)}, u32[]{:S(2)}) collective-permute-start(f32[24,8,128]{2,1,0:T(8,128)S(1)} %collective-permute-done.1.refs_2_), channel_id=1, source_target_pairs={{0,2},{2,0},{4,6},{6,4},{8,10},{10,8},{12,14},{14,12},{16,18},{18,... | collective-permute-start | bytes 294920 | tf_op jit(solution)/shard_map/ppermute | solution.py:296
  9.2 1.3 %copy-start.1 = (f32[24,8,128]{2,1,0:T(8,128)}, f32[24,8,128]{2,1,0:T(8,128)S(1)}, u32[]{:S(2)}) copy-start(f32[24,8,128]{2,1,0:T(8,128)S(1)} %collective-permute-done.refs_1_) | copy-start | bytes 294916
  10.5 0.6 %copy-start.2 = (f32[24,8,128]{2,1,0:T(8,128)}, f32[24,8,128]{2,1,0:T(8,128)S(1)}, u32[]{:S(2)}) copy-start(f32[24,8,128]{2,1,0:T(8,128)S(1)} %collective-permute-done.2.refs_3_) | copy-start | bytes 294916
  13.0 10.5 %collective-permute-start.4 = (f32[24,8,128]{2,1,0:T(8,128)}, f32[24,8,128]{2,1,0:T(8,128)S(1)}, u32[]{:S(2)}, u32[]{:S(2)}) collective-permute-start(f32[24,8,128]{2,1,0:T(8,128)} %shard_map.96.refs_4_), channel_id=1, source_target_pairs={{0,16},{4,20},{8,24},{12,28},{16,0},{20,4},{24,8},{28,12},{1,17},{... | collective-permute-start | bytes 294920 | tf_op jit(solution)/shard_map/ppermute | solution.py:309
  17.7 5.8 %collective-permute-start.5 = (f32[24,8,128]{2,1,0:T(8,128)}, f32[24,8,128]{2,1,0:T(8,128)S(1)}, u32[]{:S(2)}, u32[]{:S(2)}) collective-permute-start(f32[24,8,128]{2,1,0:T(8,128)} %shard_map.96.refs_4_), channel_id=1, source_target_pairs={{2,26},{6,30},{10,18},{14,22},{18,10},{22,14},{26,2},{30,6},{3,27}... | collective-permute-start | bytes 294920 | tf_op jit(solution)/shard_map/ppermute | solution.py:309
  18.4 6.7 %collective-permute-start.3 = (f32[24,8,128]{2,1,0:T(8,128)}, f32[24,8,128]{2,1,0:T(8,128)S(1)}, u32[]{:S(2)}, u32[]{:S(2)}) collective-permute-start(f32[24,8,128]{2,1,0:T(8,128)} %shard_map.96.refs_4_), channel_id=1, source_target_pairs={{0,8},{4,12},{8,0},{12,4},{16,24},{20,28},{24,16},{28,20},{1,9},{5... | collective-permute-start | bytes 294920 | tf_op jit(solution)/shard_map/ppermute | solution.py:309
  23.5 1.6 %copy-start.5 = (f32[24,8,128]{2,1,0:T(8,128)}, f32[24,8,128]{2,1,0:T(8,128)S(1)}, u32[]{:S(2)}) copy-start(f32[24,8,128]{2,1,0:T(8,128)S(1)} %collective-permute-done.4.refs_6_) | copy-start | bytes 294916
  23.5 2.2 %collective-permute-start.7 = (f32[24,8,128]{2,1,0:T(8,128)S(1)}, f32[24,8,128]{2,1,0:T(8,128)S(1)}, u32[]{:S(2)}, u32[]{:S(2)}) collective-permute-start(f32[24,8,128]{2,1,0:T(8,128)S(1)} %collective-permute-done.4.refs_6_), channel_id=1, source_target_pairs={{0,2},{2,0},{4,6},{6,4},{8,10},{10,8},{12,14},{14,12},{16,18},{18,... | collective-permute-start | bytes 294920 | tf_op jit(solution)/shard_map/ppermute | solution.py:296
  23.6 1.6 %copy-start.3 = (f32[24,8,128]{2,1,0:T(8,128)}, f32[24,8,128]{2,1,0:T(8,128)S(1)}, u32[]{:S(2)}) copy-start(f32[24,8,128]{2,1,0:T(8,128)S(1)} %collective-permute-done.5.refs_7_) | copy-start | bytes 294916
  25.1 0.6 %copy-start.4 = (f32[24,8,128]{2,1,0:T(8,128)}, f32[24,8,128]{2,1,0:T(8,128)S(1)}, u32[]{:S(2)}) copy-start(f32[24,8,128]{2,1,0:T(8,128)S(1)} %collective-permute-done.3.refs_5_) | copy-start | bytes 294916
  25.8 1.3 %collective-permute-start.6 = (f32[24,8,128]{2,1,0:T(8,128)S(1)}, f32[24,8,128]{2,1,0:T(8,128)S(1)}, u32[]{:S(2)}, u32[]{:S(2)}) collective-permute-start(f32[24,8,128]{2,1,0:T(8,128)S(1)} %add.9), channel_id=1, source_target_pairs={{0,2},{2,0},{4,6},{6,4},{8,10},{10,8},{12,14},{14,12},{16,18},{18,... | collective-permute-start | bytes 294920 | tf_op jit(solution)/shard_map/ppermute | solution.py:296
  25.8 1.3 %copy-start.6 = (f32[24,8,128]{2,1,0:T(8,128)}, f32[24,8,128]{2,1,0:T(8,128)S(1)}, u32[]{:S(2)}) copy-start(f32[24,8,128]{2,1,0:T(8,128)S(1)} %collective-permute-done.7.refs_9_) | copy-start | bytes 294916
  27.1 0.6 %copy-start.7 = (f32[24,8,128]{2,1,0:T(8,128)}, f32[24,8,128]{2,1,0:T(8,128)S(1)}, u32[]{:S(2)}) copy-start(f32[24,8,128]{2,1,0:T(8,128)S(1)} %collective-permute-done.6.refs_8_) | copy-start | bytes 294916
  31.2 4.5 %collective-permute-start.8 = (f32[2,16,512]{2,1,0:T(8,128)}, f32[2,16,512]{2,1,0:T(8,128)S(1)}, u32[]{:S(2)}, u32[]{:S(2)}) collective-permute-start(f32[2,16,512]{2,1,0:T(8,128)} %get-tuple-element.6), channel_id=1, source_target_pairs={{0,1},{1,0},{2,3},{3,2},{4,5},{5,4},{6,7},{7,6},{8,9},{9,8},{10,11... | collective-permute-start | bytes 196616 | tf_op jit(solution)/shard_map/ppermute | solution.py:349
